TPU v7x, 512 devices: a whole 4x8x8 slice. The times are simulated.
512 devices in a mesh: seg: 32 (over y, x), sec: 16 (over z, core).
Axes of the slice: x: 4, y: 8, z: 8, core: 2. Of those that a mesh axis runs over, the one named last changes fastest.
Arguments:
- blocks: bfloat16 [32, 4, 16, 128, 128], P('seg', None, 'sec'), may hold values from -0.5 to 0.5
- left_edge: bfloat16 [16, 128], P('sec'), may hold values from -0.5 to 0.5
- right_edge: bfloat16 [16, 128], P('sec'), may hold values from -6 to 6
- occupation: int32 [1024, 32], P(None, 'seg'), may hold values from 0 to 3
- start_sector: int32 [1024], replicated, may hold values from 0 to 15
Outputs:
- amplitude: float32 [1024], replicated
All inputs are finite; a program needn't handle non-finite values.
Results may differ from a plain program's by a relative error of at most 0.015.
Values may be sent and summed in bfloat16 or wider, within the bound.
No kernel may reach another device: no remote copies, remote signals or barrier semaphores. Data moves between devices by JAX's collectives and lax.ppermute only.
A program may use at most 64 MiB of HBM per device.

v0:
```python
import jax
import jax.numpy as jnp
from jax import lax
from jax.sharding import PartitionSpec as P


def padded_2(block, sides, width, periodic):
    for axis, dim in sides:
        count = lax.axis_size(axis)
        forward = [(i, i + 1) for i in range(count - 1)]
        if periodic:
            forward.append((count - 1, 0))
        backward = [(target, source) for source, target in forward]
        low = lax.ppermute(
            lax.slice_in_dim(block, block.shape[dim] - width, None, axis=dim), axis, forward
        )
        high = lax.ppermute(lax.slice_in_dim(block, 0, width, axis=dim), axis, backward)
        block = jnp.concatenate([low, block, high], axis=dim)
    return block


def state_masks(occ_site):
    levels = jnp.arange(4, dtype=jnp.int32)
    return (occ_site[:, None] == levels[None, :]).astype(jnp.float32)


def forward_send(vector, block_site, occ_masks):
    products = jnp.einsum("ka,nab->knb", vector, block_site, preferred_element_type=jnp.float32)
    terms = products * occ_masks[:, :, None]
    kept_term = (terms[:, 0] + terms[:, 3]).astype(jnp.bfloat16)
    upward = terms[:, 1].astype(jnp.bfloat16)
    downward = terms[:, 2].astype(jnp.bfloat16)
    return (kept_term, jnp.stack([downward, upward]))


def backward_send(vector, block_site, occ_masks):
    return (vector, jnp.stack([vector, vector]))


def forward_take(kept_term, padded, block_site, occ_masks):
    total = (
        kept_term.astype(jnp.float32)
        + padded[0].astype(jnp.float32)
        + padded[3].astype(jnp.float32)
    )
    return total.astype(jnp.bfloat16)


def backward_take(kept_term, padded, block_site, occ_masks):
    stacked = jnp.stack([kept_term, padded[3], padded[0], kept_term], axis=1)
    products = jnp.einsum("nab,knb->kna", block_site, stacked, preferred_element_type=jnp.float32)
    return jnp.sum(products * occ_masks[:, :, None], axis=1).astype(jnp.bfloat16)


def per_device(blocks, left_edge, right_edge, occupation, start_sector):
    seg_count = lax.axis_size("seg")
    half_count = seg_count // 2
    seg_index = lax.axis_index("seg")
    sec_index = lax.axis_index("sec")
    is_left = seg_index < half_count
    chain_depth = jnp.where(is_left, seg_index, seg_count - 1 - seg_index)
    is_first = chain_depth == 0
    meet_lower = seg_index == half_count - 1
    meet_upper = seg_index == half_count
    conf_count = occupation.shape[0]
    sites_here = occupation.shape[1]
    sector_width = blocks.shape[-1]
    block_count = 1
    columns = jnp.arange(sector_width, dtype=jnp.int32)
    lower_cols = (columns < sector_width // 2).astype(jnp.float32)
    upper_cols = 1.0 - lower_cols
    local_blocks = blocks[:, :, 0]
    left_row = left_edge[0]
    right_row = right_edge[0]
    batch_rows = conf_count // block_count

    def initial():
        zero_row = jnp.zeros_like(left_row)
        initial_left = jnp.where(
            (start_sector == sec_index)[:, None], left_row[None, :], zero_row[None, :]
        )
        initial_right = jnp.broadcast_to(right_row[None, :], (batch_rows, sector_width))
        return jnp.where(is_left, initial_left, initial_right)

    def run_sites(vector):
        position = jnp.where(is_left, 0, sites_here - 1)
        block_site = lax.dynamic_index_in_dim(local_blocks, position, 0, keepdims=False)
        occ_site = lax.dynamic_index_in_dim(occupation, position, 1, keepdims=False)
        occ_masks = state_masks(occ_site)
        kept_term, outgoing = lax.cond(
            is_left, forward_send, backward_send, vector, block_site, occ_masks
        )
        padded = padded_2(outgoing, (("sec", 0),), 1, True)
        vector = lax.cond(
            is_left, forward_take, backward_take, kept_term, padded, block_site, occ_masks
        )
        return vector

    section_count = half_count + block_count - 1

    def section(section_index, state_pair):
        incoming, partial_value = state_pair
        batch_index = section_index - chain_depth
        is_valid = (batch_index >= 0) & (batch_index < block_count)
        vector = jnp.where(is_first, initial(), incoming)
        vector = run_sites(vector)
        padded = padded_2(vector[None], (("seg", 0),), 1, False)
        received = jnp.where(is_left, padded[0], padded[2])
        own_vals = vector.astype(jnp.float32)
        lower_part = jnp.sum(own_vals * padded[2].astype(jnp.float32) * lower_cols[None, :], axis=1)
        upper_part = jnp.sum(own_vals * padded[0].astype(jnp.float32) * upper_cols[None, :], axis=1)
        product = jnp.where(meet_lower, lower_part, upper_part)
        previous = partial_value
        store_here = (meet_lower | meet_upper) & is_valid
        partial_value = jnp.where(store_here, product, previous)
        return (received, partial_value)

    start_state = (
        jnp.zeros((batch_rows, sector_width), jnp.bfloat16),
        jnp.zeros((conf_count,), jnp.float32),
    )
    final_state = lax.fori_loop(0, section_count, section, start_state)
    return lax.psum(final_state[1], ("seg", "sec"))


def solution(mesh):
    in_specs = (
        P("seg", None, "sec", None, None),
        P("sec", None),
        P("sec", None),
        P(None, "seg"),
        P(),
    )
    out_specs = P()
    return jax.shard_map(
        per_device, mesh=mesh, in_specs=in_specs, out_specs=out_specs, check_vma=False
    )
```

profile of v0, /device:TPU:1, one launch (start us, length us, event | category | flops | bytes accessed | tf_op | source)
XLA Modules:
  0.0 528.2 jit_solution(16015874300515925806)
XLA Ops:
  0.0 413.8 %while.18 = (s32[]{:T(128)}, bf16[1024,128]{1,0:T(8,128)(2,1)S(1)}, f32[1024]{0:T(1024)S(1)}, pred[]{:T(512)}, pred[]{:T(512)}, /*index=5*/s32[]{:T(128)}, s32[1...) while((s32[]{:T(128)}, bf16[1024,128]{1,0:T(8,128)(2,1)S(1)}, ...), condition=%wide.region_8.9_spmd.clone, body=%wide.region_0.8_spmd.clone.sunk | while | flops 274213504 | bytes 16602105 | solution.py:122
  4.2 6.8 %collective-permute-start = (bf16[1,1024,128]{2,1,0:T(8,128)(2,1)S(1)}, bf16[1,1024,128]{2,1,0:T(8,128)(2,1)S(1)}, u32[]{:S(2)}, u32[]{:S(2)}) collective-permute-start(bf16[1,1024,128]{2,1,0:T(8,128)(2,1)S(1)} %get-tuple-element.627), channel_id=1, source_target_pairs={{1,0},{2,1},{3,2},{4,3},{5,4},{6,5},{7,6},{8,7},{9,8},{10,9},{11,1... | collective-permute-start | bytes 786440 | tf_op jit(solution)/shard_map/while/body/eval_jaxpr/ppermute | solution.py:17
  12.2 3.0 collective-permute-done.1
  15.3 3.1 collective-permute-start.2
  19.8 1.9 collective-permute-done.2
  21.7 3.8 collective-permute-done.3
  30.1 7.4 %collective-permute-start = (bf16[1,1024,128]{2,1,0:T(8,128)(2,1)S(1)}, bf16[1,1024,128]{2,1,0:T(8,128)(2,1)S(1)}, u32[]{:S(2)}, u32[]{:S(2)}) collective-permute-start(bf16[1,1024,128]{2,1,0:T(8,128)(2,1)S(1)} %get-tuple-element.627), channel_id=1, source_target_pairs={{1,0},{2,1},{3,2},{4,3},{5,4},{6,5},{7,6},{8,7},{9,8},{10,9},{11,1... | collective-permute-start | bytes 786440 | tf_op jit(solution)/shard_map/while/body/eval_jaxpr/ppermute | solution.py:17
  38.7 2.2 collective-permute-done.1
  41.0 3.1 collective-permute-start.2
  45.5 1.9 collective-permute-done.2
  47.4 3.8 collective-permute-done.3
  55.8 6.6 %collective-permute-start = (bf16[1,1024,128]{2,1,0:T(8,128)(2,1)S(1)}, bf16[1,1024,128]{2,1,0:T(8,128)(2,1)S(1)}, u32[]{:S(2)}, u32[]{:S(2)}) collective-permute-start(bf16[1,1024,128]{2,1,0:T(8,128)(2,1)S(1)} %get-tuple-element.627), channel_id=1, source_target_pairs={{1,0},{2,1},{3,2},{4,3},{5,4},{6,5},{7,6},{8,7},{9,8},{10,9},{11,1... | collective-permute-start | bytes 786440 | tf_op jit(solution)/shard_map/while/body/eval_jaxpr/ppermute | solution.py:17
  65.8 4.4 collective-permute-start.2
  73.5 4.1 collective-permute-done.3
  82.1 6.6 %collective-permute-start = (bf16[1,1024,128]{2,1,0:T(8,128)(2,1)S(1)}, bf16[1,1024,128]{2,1,0:T(8,128)(2,1)S(1)}, u32[]{:S(2)}, u32[]{:S(2)}) collective-permute-start(bf16[1,1024,128]{2,1,0:T(8,128)(2,1)S(1)} %get-tuple-element.627), channel_id=1, source_target_pairs={{1,0},{2,1},{3,2},{4,3},{5,4},{6,5},{7,6},{8,7},{9,8},{10,9},{11,1... | collective-permute-start | bytes 786440 | tf_op jit(solution)/shard_map/while/body/eval_jaxpr/ppermute | solution.py:17
  89.9 2.2 collective-permute-done.1
  92.2 3.8 collective-permute-start.2
  97.3 1.9 collective-permute-done.2
  99.2 4.1 collective-permute-done.3
  107.9 6.4 %collective-permute-start = (bf16[1,1024,128]{2,1,0:T(8,128)(2,1)S(1)}, bf16[1,1024,128]{2,1,0:T(8,128)(2,1)S(1)}, u32[]{:S(2)}, u32[]{:S(2)}) collective-permute-start(bf16[1,1024,128]{2,1,0:T(8,128)(2,1)S(1)} %get-tuple-element.627), channel_id=1, source_target_pairs={{1,0},{2,1},{3,2},{4,3},{5,4},{6,5},{7,6},{8,7},{9,8},{10,9},{11,1... | collective-permute-start | bytes 786440 | tf_op jit(solution)/shard_map/while/body/eval_jaxpr/ppermute | solution.py:17
  115.6 2.0 collective-permute-done.1
  117.8 3.7 collective-permute-start.2
  122.8 1.9 collective-permute-done.2
  124.7 4.0 collective-permute-done.3
  133.2 6.4 %collective-permute-start = (bf16[1,1024,128]{2,1,0:T(8,128)(2,1)S(1)}, bf16[1,1024,128]{2,1,0:T(8,128)(2,1)S(1)}, u32[]{:S(2)}, u32[]{:S(2)}) collective-permute-start(bf16[1,1024,128]{2,1,0:T(8,128)(2,1)S(1)} %get-tuple-element.627), channel_id=1, source_target_pairs={{1,0},{2,1},{3,2},{4,3},{5,4},{6,5},{7,6},{8,7},{9,8},{10,9},{11,1... | collective-permute-start | bytes 786440 | tf_op jit(solution)/shard_map/while/body/eval_jaxpr/ppermute | solution.py:17
  143.1 3.6 collective-permute-start.2
  148.0 1.9 collective-permute-done.2
  149.9 4.0 collective-permute-done.3
  158.5 6.3 %collective-permute-start = (bf16[1,1024,128]{2,1,0:T(8,128)(2,1)S(1)}, bf16[1,1024,128]{2,1,0:T(8,128)(2,1)S(1)}, u32[]{:S(2)}, u32[]{:S(2)}) collective-permute-start(bf16[1,1024,128]{2,1,0:T(8,128)(2,1)S(1)} %get-tuple-element.627), channel_id=1, source_target_pairs={{1,0},{2,1},{3,2},{4,3},{5,4},{6,5},{7,6},{8,7},{9,8},{10,9},{11,1... | collective-permute-start | bytes 786440 | tf_op jit(solution)/shard_map/while/body/eval_jaxpr/ppermute | solution.py:17
  168.3 3.6 collective-permute-start.2
  175.1 4.1 collective-permute-done.3
  183.7 6.3 %collective-permute-start = (bf16[1,1024,128]{2,1,0:T(8,128)(2,1)S(1)}, bf16[1,1024,128]{2,1,0:T(8,128)(2,1)S(1)}, u32[]{:S(2)}, u32[]{:S(2)}) collective-permute-start(bf16[1,1024,128]{2,1,0:T(8,128)(2,1)S(1)} %get-tuple-element.627), channel_id=1, source_target_pairs={{1,0},{2,1},{3,2},{4,3},{5,4},{6,5},{7,6},{8,7},{9,8},{10,9},{11,1... | collective-permute-start | bytes 786440 | tf_op jit(solution)/shard_map/while/body/eval_jaxpr/ppermute | solution.py:17
  193.4 3.6 collective-permute-start.2
  200.3 4.1 collective-permute-done.3
  208.9 6.2 %collective-permute-start = (bf16[1,1024,128]{2,1,0:T(8,128)(2,1)S(1)}, bf16[1,1024,128]{2,1,0:T(8,128)(2,1)S(1)}, u32[]{:S(2)}, u32[]{:S(2)}) collective-permute-start(bf16[1,1024,128]{2,1,0:T(8,128)(2,1)S(1)} %get-tuple-element.627), channel_id=1, source_target_pairs={{1,0},{2,1},{3,2},{4,3},{5,4},{6,5},{7,6},{8,7},{9,8},{10,9},{11,1... | collective-permute-start | bytes 786440 | tf_op jit(solution)/shard_map/while/body/eval_jaxpr/ppermute | solution.py:17
  218.6 3.6 collective-permute-start.2
  225.5 4.1 collective-permute-done.3
  234.1 6.2 %collective-permute-start = (bf16[1,1024,128]{2,1,0:T(8,128)(2,1)S(1)}, bf16[1,1024,128]{2,1,0:T(8,128)(2,1)S(1)}, u32[]{:S(2)}, u32[]{:S(2)}) collective-permute-start(bf16[1,1024,128]{2,1,0:T(8,128)(2,1)S(1)} %get-tuple-element.627), channel_id=1, source_target_pairs={{1,0},{2,1},{3,2},{4,3},{5,4},{6,5},{7,6},{8,7},{9,8},{10,9},{11,1... | collective-permute-start | bytes 786440 | tf_op jit(solution)/shard_map/while/body/eval_jaxpr/ppermute | solution.py:17
  243.7 3.6 collective-permute-start.2
  250.6 4.1 collective-permute-done.3
  259.2 6.2 %collective-permute-start = (bf16[1,1024,128]{2,1,0:T(8,128)(2,1)S(1)}, bf16[1,1024,128]{2,1,0:T(8,128)(2,1)S(1)}, u32[]{:S(2)}, u32[]{:S(2)}) collective-permute-start(bf16[1,1024,128]{2,1,0:T(8,128)(2,1)S(1)} %get-tuple-element.627), channel_id=1, source_target_pairs={{1,0},{2,1},{3,2},{4,3},{5,4},{6,5},{7,6},{8,7},{9,8},{10,9},{11,1... | collective-permute-start | bytes 786440 | tf_op jit(solution)/shard_map/while/body/eval_jaxpr/ppermute | solution.py:17
  268.8 3.8 collective-permute-start.2
  273.9 1.9 collective-permute-done.2
  275.9 4.4 collective-permute-done.3
  284.8 6.2 %collective-permute-start = (bf16[1,1024,128]{2,1,0:T(8,128)(2,1)S(1)}, bf16[1,1024,128]{2,1,0:T(8,128)(2,1)S(1)}, u32[]{:S(2)}, u32[]{:S(2)}) collective-permute-start(bf16[1,1024,128]{2,1,0:T(8,128)(2,1)S(1)} %get-tuple-element.627), channel_id=1, source_target_pairs={{1,0},{2,1},{3,2},{4,3},{5,4},{6,5},{7,6},{8,7},{9,8},{10,9},{11,1... | collective-permute-start | bytes 786440 | tf_op jit(solution)/shard_map/while/body/eval_jaxpr/ppermute | solution.py:17
  294.4 6.0 %collective-permute-start.2 = (bf16[1,1024,128]{2,1,0:T(8,128)(2,1)S(1)}, bf16[1,1024,128]{2,1,0:T(8,128)(2,1)S(1)}, u32[]{:S(2)}, u32[]{:S(2)}) collective-permute-start(bf16[1,1024,128]{2,1,0:T(8,128)(2,1)S(1)} %bitcast.59), channel_id=1, source_target_pairs={{0,16},{16,32},{32,48},{48,64},{64,80},{80,96},{96,112},{112,128},... | collective-permute-start | bytes 786440 | tf_op jit(solution)/shard_map/while/body/eval_jaxpr/ppermute | solution.py:14
  303.7 4.1 collective-permute-done.3
  312.3 6.4 %collective-permute-start = (bf16[1,1024,128]{2,1,0:T(8,128)(2,1)S(1)}, bf16[1,1024,128]{2,1,0:T(8,128)(2,1)S(1)}, u32[]{:S(2)}, u32[]{:S(2)}) collective-permute-start(bf16[1,1024,128]{2,1,0:T(8,128)(2,1)S(1)} %get-tuple-element.627), channel_id=1, source_target_pairs={{1,0},{2,1},{3,2},{4,3},{5,4},{6,5},{7,6},{8,7},{9,8},{10,9},{11,1... | collective-permute-start | bytes 786440 | tf_op jit(solution)/shard_map/while/body/eval_jaxpr/ppermute | solution.py:17
  320.0 2.0 collective-permute-done.1
  322.2 4.7 collective-permute-start.2
  330.1 4.1 collective-permute-done.3
  338.8 6.4 %collective-permute-start = (bf16[1,1024,128]{2,1,0:T(8,128)(2,1)S(1)}, bf16[1,1024,128]{2,1,0:T(8,128)(2,1)S(1)}, u32[]{:S(2)}, u32[]{:S(2)}) collective-permute-start(bf16[1,1024,128]{2,1,0:T(8,128)(2,1)S(1)} %get-tuple-element.627), channel_id=1, source_target_pairs={{1,0},{2,1},{3,2},{4,3},{5,4},{6,5},{7,6},{8,7},{9,8},{10,9},{11,1... | collective-permute-start | bytes 786440 | tf_op jit(solution)/shard_map/while/body/eval_jaxpr/ppermute | solution.py:17
  346.5 2.0 collective-permute-done.1
  348.6 4.6 collective-permute-start.2
  356.5 4.1 collective-permute-done.3
  365.2 6.4 %collective-permute-start = (bf16[1,1024,128]{2,1,0:T(8,128)(2,1)S(1)}, bf16[1,1024,128]{2,1,0:T(8,128)(2,1)S(1)}, u32[]{:S(2)}, u32[]{:S(2)}) collective-permute-start(bf16[1,1024,128]{2,1,0:T(8,128)(2,1)S(1)} %get-tuple-element.627), channel_id=1, source_target_pairs={{1,0},{2,1},{3,2},{4,3},{5,4},{6,5},{7,6},{8,7},{9,8},{10,9},{11,1... | collective-permute-start | bytes 786440 | tf_op jit(solution)/shard_map/while/body/eval_jaxpr/ppermute | solution.py:17
  372.9 2.0 collective-permute-done.1
  375.0 4.7 collective-permute-start.2
  383.0 4.1 collective-permute-done.3
  391.6 6.4 %collective-permute-start = (bf16[1,1024,128]{2,1,0:T(8,128)(2,1)S(1)}, bf16[1,1024,128]{2,1,0:T(8,128)(2,1)S(1)}, u32[]{:S(2)}, u32[]{:S(2)}) collective-permute-start(bf16[1,1024,128]{2,1,0:T(8,128)(2,1)S(1)} %get-tuple-element.627), channel_id=1, source_target_pairs={{1,0},{2,1},{3,2},{4,3},{5,4},{6,5},{7,6},{8,7},{9,8},{10,9},{11,1... | collective-permute-start | bytes 786440 | tf_op jit(solution)/shard_map/while/body/eval_jaxpr/ppermute | solution.py:17
  399.3 2.0 collective-permute-done.1
  401.5 4.6 collective-permute-start.2
  409.3 4.1 collective-permute-done.3
  413.8 114.3 %psum.7 = f32[1024]{0:T(1024)} all-reduce(f32[1024]{0:T(1024)S(1)} %get-tuple-element.425), channel_id=1, replica_groups=mesh['seg'=32,'sec'=16] {'seg','sec'}, use_global_device_ids=true, to_apply=%region_9.10 | all-reduce | flops 1024 | bytes 8192 | tf_op jit(solution)/shard_map/psum | solution.py:123
  (324 shorter events, 180.4 us)
Async XLA Ops:
  4.2 8.0 %collective-permute-start = (bf16[1,1024,128]{2,1,0:T(8,128)(2,1)S(1)}, bf16[1,1024,128]{2,1,0:T(8,128)(2,1)S(1)}, u32[]{:S(2)}, u32[]{:S(2)}) collective-permute-start(bf16[1,1024,128]{2,1,0:T(8,128)(2,1)S(1)} %get-tuple-element.627), channel_id=1, source_target_pairs={{1,0},{2,1},{3,2},{4,3},{5,4},{6,5},{7,6},{8,7},{9,8},{10,9},{11,1... | collective-permute-start | bytes 786440 | tf_op jit(solution)/shard_map/while/body/eval_jaxpr/ppermute | solution.py:17
  11.0 4.2 collective-permute-start.1
  15.3 6.4 %collective-permute-start.2 = (bf16[1,1024,128]{2,1,0:T(8,128)(2,1)S(1)}, bf16[1,1024,128]{2,1,0:T(8,128)(2,1)S(1)}, u32[]{:S(2)}, u32[]{:S(2)}) collective-permute-start(bf16[1,1024,128]{2,1,0:T(8,128)(2,1)S(1)} %bitcast.59), channel_id=1, source_target_pairs={{0,16},{16,32},{32,48},{48,64},{64,80},{80,96},{96,112},{112,128},... | collective-permute-start | bytes 786440 | tf_op jit(solution)/shard_map/while/body/eval_jaxpr/ppermute | solution.py:14
  18.5 7.1 %collective-permute-start.3 = (bf16[1,1024,128]{2,1,0:T(8,128)(2,1)S(1)}, bf16[1,1024,128]{2,1,0:T(8,128)(2,1)S(1)}, u32[]{:S(2)}, u32[]{:S(2)}) collective-permute-start(bf16[1,1024,128]{2,1,0:T(8,128)(2,1)S(1)} %bitcast.60), channel_id=1, source_target_pairs={{16,0},{32,16},{48,32},{64,48},{80,64},{96,80},{112,96},{128,112},... | collective-permute-start | bytes 786440 | tf_op jit(solution)/shard_map/while/body/eval_jaxpr/ppermute | solution.py:17
  30.1 8.6 %collective-permute-start = (bf16[1,1024,128]{2,1,0:T(8,128)(2,1)S(1)}, bf16[1,1024,128]{2,1,0:T(8,128)(2,1)S(1)}, u32[]{:S(2)}, u32[]{:S(2)}) collective-permute-start(bf16[1,1024,128]{2,1,0:T(8,128)(2,1)S(1)} %get-tuple-element.627), channel_id=1, source_target_pairs={{1,0},{2,1},{3,2},{4,3},{5,4},{6,5},{7,6},{8,7},{9,8},{10,9},{11,1... | collective-permute-start | bytes 786440 | tf_op jit(solution)/shard_map/while/body/eval_jaxpr/ppermute | solution.py:17
  37.6 3.3 collective-permute-start.1
  41.0 6.4 %collective-permute-start.2 = (bf16[1,1024,128]{2,1,0:T(8,128)(2,1)S(1)}, bf16[1,1024,128]{2,1,0:T(8,128)(2,1)S(1)}, u32[]{:S(2)}, u32[]{:S(2)}) collective-permute-start(bf16[1,1024,128]{2,1,0:T(8,128)(2,1)S(1)} %bitcast.59), channel_id=1, source_target_pairs={{0,16},{16,32},{32,48},{48,64},{64,80},{80,96},{96,112},{112,128},... | collective-permute-start | bytes 786440 | tf_op jit(solution)/shard_map/while/body/eval_jaxpr/ppermute | solution.py:14
  44.1 7.1 %collective-permute-start.3 = (bf16[1,1024,128]{2,1,0:T(8,128)(2,1)S(1)}, bf16[1,1024,128]{2,1,0:T(8,128)(2,1)S(1)}, u32[]{:S(2)}, u32[]{:S(2)}) collective-permute-start(bf16[1,1024,128]{2,1,0:T(8,128)(2,1)S(1)} %bitcast.60), channel_id=1, source_target_pairs={{16,0},{32,16},{48,32},{64,48},{80,64},{96,80},{112,96},{128,112},... | collective-permute-start | bytes 786440 | tf_op jit(solution)/shard_map/while/body/eval_jaxpr/ppermute | solution.py:17
  55.8 8.0 %collective-permute-start = (bf16[1,1024,128]{2,1,0:T(8,128)(2,1)S(1)}, bf16[1,1024,128]{2,1,0:T(8,128)(2,1)S(1)}, u32[]{:S(2)}, u32[]{:S(2)}) collective-permute-start(bf16[1,1024,128]{2,1,0:T(8,128)(2,1)S(1)} %get-tuple-element.627), channel_id=1, source_target_pairs={{1,0},{2,1},{3,2},{4,3},{5,4},{6,5},{7,6},{8,7},{9,8},{10,9},{11,1... | collective-permute-start | bytes 786440 | tf_op jit(solution)/shard_map/while/body/eval_jaxpr/ppermute | solution.py:17
  62.4 3.3 collective-permute-start.1
  65.8 7.7 %collective-permute-start.2 = (bf16[1,1024,128]{2,1,0:T(8,128)(2,1)S(1)}, bf16[1,1024,128]{2,1,0:T(8,128)(2,1)S(1)}, u32[]{:S(2)}, u32[]{:S(2)}) collective-permute-start(bf16[1,1024,128]{2,1,0:T(8,128)(2,1)S(1)} %bitcast.59), channel_id=1, source_target_pairs={{0,16},{16,32},{32,48},{48,64},{64,80},{80,96},{96,112},{112,128},... | collective-permute-start | bytes 786440 | tf_op jit(solution)/shard_map/while/body/eval_jaxpr/ppermute | solution.py:14
  70.2 7.4 %collective-permute-start.3 = (bf16[1,1024,128]{2,1,0:T(8,128)(2,1)S(1)}, bf16[1,1024,128]{2,1,0:T(8,128)(2,1)S(1)}, u32[]{:S(2)}, u32[]{:S(2)}) collective-permute-start(bf16[1,1024,128]{2,1,0:T(8,128)(2,1)S(1)} %bitcast.60), channel_id=1, source_target_pairs={{16,0},{32,16},{48,32},{64,48},{80,64},{96,80},{112,96},{128,112},... | collective-permute-start | bytes 786440 | tf_op jit(solution)/shard_map/while/body/eval_jaxpr/ppermute | solution.py:17
  82.1 7.8 %collective-permute-start = (bf16[1,1024,128]{2,1,0:T(8,128)(2,1)S(1)}, bf16[1,1024,128]{2,1,0:T(8,128)(2,1)S(1)}, u32[]{:S(2)}, u32[]{:S(2)}) collective-permute-start(bf16[1,1024,128]{2,1,0:T(8,128)(2,1)S(1)} %get-tuple-element.627), channel_id=1, source_target_pairs={{1,0},{2,1},{3,2},{4,3},{5,4},{6,5},{7,6},{8,7},{9,8},{10,9},{11,1... | collective-permute-start | bytes 786440 | tf_op jit(solution)/shard_map/while/body/eval_jaxpr/ppermute | solution.py:17
  88.8 3.3 collective-permute-start.1
  92.2 7.0 %collective-permute-start.2 = (bf16[1,1024,128]{2,1,0:T(8,128)(2,1)S(1)}, bf16[1,1024,128]{2,1,0:T(8,128)(2,1)S(1)}, u32[]{:S(2)}, u32[]{:S(2)}) collective-permute-start(bf16[1,1024,128]{2,1,0:T(8,128)(2,1)S(1)} %bitcast.59), channel_id=1, source_target_pairs={{0,16},{16,32},{32,48},{48,64},{64,80},{80,96},{96,112},{112,128},... | collective-permute-start | bytes 786440 | tf_op jit(solution)/shard_map/while/body/eval_jaxpr/ppermute | solution.py:14
  96.0 7.4 %collective-permute-start.3 = (bf16[1,1024,128]{2,1,0:T(8,128)(2,1)S(1)}, bf16[1,1024,128]{2,1,0:T(8,128)(2,1)S(1)}, u32[]{:S(2)}, u32[]{:S(2)}) collective-permute-start(bf16[1,1024,128]{2,1,0:T(8,128)(2,1)S(1)} %bitcast.60), channel_id=1, source_target_pairs={{16,0},{32,16},{48,32},{64,48},{80,64},{96,80},{112,96},{128,112},... | collective-permute-start | bytes 786440 | tf_op jit(solution)/shard_map/while/body/eval_jaxpr/ppermute | solution.py:17
  107.9 7.7 %collective-permute-start = (bf16[1,1024,128]{2,1,0:T(8,128)(2,1)S(1)}, bf16[1,1024,128]{2,1,0:T(8,128)(2,1)S(1)}, u32[]{:S(2)}, u32[]{:S(2)}) collective-permute-start(bf16[1,1024,128]{2,1,0:T(8,128)(2,1)S(1)} %get-tuple-element.627), channel_id=1, source_target_pairs={{1,0},{2,1},{3,2},{4,3},{5,4},{6,5},{7,6},{8,7},{9,8},{10,9},{11,1... | collective-permute-start | bytes 786440 | tf_op jit(solution)/shard_map/while/body/eval_jaxpr/ppermute | solution.py:17
  114.3 3.3 collective-permute-start.1
  117.8 7.0 %collective-permute-start.2 = (bf16[1,1024,128]{2,1,0:T(8,128)(2,1)S(1)}, bf16[1,1024,128]{2,1,0:T(8,128)(2,1)S(1)}, u32[]{:S(2)}, u32[]{:S(2)}) collective-permute-start(bf16[1,1024,128]{2,1,0:T(8,128)(2,1)S(1)} %bitcast.59), channel_id=1, source_target_pairs={{0,16},{16,32},{32,48},{48,64},{64,80},{80,96},{96,112},{112,128},... | collective-permute-start | bytes 786440 | tf_op jit(solution)/shard_map/while/body/eval_jaxpr/ppermute | solution.py:14
  121.4 7.2 %collective-permute-start.3 = (bf16[1,1024,128]{2,1,0:T(8,128)(2,1)S(1)}, bf16[1,1024,128]{2,1,0:T(8,128)(2,1)S(1)}, u32[]{:S(2)}, u32[]{:S(2)}) collective-permute-start(bf16[1,1024,128]{2,1,0:T(8,128)(2,1)S(1)} %bitcast.60), channel_id=1, source_target_pairs={{16,0},{32,16},{48,32},{64,48},{80,64},{96,80},{112,96},{128,112},... | collective-permute-start | bytes 786440 | tf_op jit(solution)/shard_map/while/body/eval_jaxpr/ppermute | solution.py:17
  133.2 7.9 %collective-permute-start = (bf16[1,1024,128]{2,1,0:T(8,128)(2,1)S(1)}, bf16[1,1024,128]{2,1,0:T(8,128)(2,1)S(1)}, u32[]{:S(2)}, u32[]{:S(2)}) collective-permute-start(bf16[1,1024,128]{2,1,0:T(8,128)(2,1)S(1)} %get-tuple-element.627), channel_id=1, source_target_pairs={{1,0},{2,1},{3,2},{4,3},{5,4},{6,5},{7,6},{8,7},{9,8},{10,9},{11,1... | collective-permute-start | bytes 786440 | tf_op jit(solution)/shard_map/while/body/eval_jaxpr/ppermute | solution.py:17
  139.6 3.3 collective-permute-start.1
  143.1 6.8 %collective-permute-start.2 = (bf16[1,1024,128]{2,1,0:T(8,128)(2,1)S(1)}, bf16[1,1024,128]{2,1,0:T(8,128)(2,1)S(1)}, u32[]{:S(2)}, u32[]{:S(2)}) collective-permute-start(bf16[1,1024,128]{2,1,0:T(8,128)(2,1)S(1)} %bitcast.59), channel_id=1, source_target_pairs={{0,16},{16,32},{32,48},{48,64},{64,80},{80,96},{96,112},{112,128},... | collective-permute-start | bytes 786440 | tf_op jit(solution)/shard_map/while/body/eval_jaxpr/ppermute | solution.py:14
  146.6 7.3 %collective-permute-start.3 = (bf16[1,1024,128]{2,1,0:T(8,128)(2,1)S(1)}, bf16[1,1024,128]{2,1,0:T(8,128)(2,1)S(1)}, u32[]{:S(2)}, u32[]{:S(2)}) collective-permute-start(bf16[1,1024,128]{2,1,0:T(8,128)(2,1)S(1)} %bitcast.60), channel_id=1, source_target_pairs={{16,0},{32,16},{48,32},{64,48},{80,64},{96,80},{112,96},{128,112},... | collective-permute-start | bytes 786440 | tf_op jit(solution)/shard_map/while/body/eval_jaxpr/ppermute | solution.py:17
  158.5 7.8 %collective-permute-start = (bf16[1,1024,128]{2,1,0:T(8,128)(2,1)S(1)}, bf16[1,1024,128]{2,1,0:T(8,128)(2,1)S(1)}, u32[]{:S(2)}, u32[]{:S(2)}) collective-permute-start(bf16[1,1024,128]{2,1,0:T(8,128)(2,1)S(1)} %get-tuple-element.627), channel_id=1, source_target_pairs={{1,0},{2,1},{3,2},{4,3},{5,4},{6,5},{7,6},{8,7},{9,8},{10,9},{11,1... | collective-permute-start | bytes 786440 | tf_op jit(solution)/shard_map/while/body/eval_jaxpr/ppermute | solution.py:17
  164.8 3.3 collective-permute-start.1
  168.3 6.9 %collective-permute-start.2 = (bf16[1,1024,128]{2,1,0:T(8,128)(2,1)S(1)}, bf16[1,1024,128]{2,1,0:T(8,128)(2,1)S(1)}, u32[]{:S(2)}, u32[]{:S(2)}) collective-permute-start(bf16[1,1024,128]{2,1,0:T(8,128)(2,1)S(1)} %bitcast.59), channel_id=1, source_target_pairs={{0,16},{16,32},{32,48},{48,64},{64,80},{80,96},{96,112},{112,128},... | collective-permute-start | bytes 786440 | tf_op jit(solution)/shard_map/while/body/eval_jaxpr/ppermute | solution.py:14
  171.8 7.3 %collective-permute-start.3 = (bf16[1,1024,128]{2,1,0:T(8,128)(2,1)S(1)}, bf16[1,1024,128]{2,1,0:T(8,128)(2,1)S(1)}, u32[]{:S(2)}, u32[]{:S(2)}) collective-permute-start(bf16[1,1024,128]{2,1,0:T(8,128)(2,1)S(1)} %bitcast.60), channel_id=1, source_target_pairs={{16,0},{32,16},{48,32},{64,48},{80,64},{96,80},{112,96},{128,112},... | collective-permute-start | bytes 786440 | tf_op jit(solution)/shard_map/while/body/eval_jaxpr/ppermute | solution.py:17
  183.7 7.8 %collective-permute-start = (bf16[1,1024,128]{2,1,0:T(8,128)(2,1)S(1)}, bf16[1,1024,128]{2,1,0:T(8,128)(2,1)S(1)}, u32[]{:S(2)}, u32[]{:S(2)}) collective-permute-start(bf16[1,1024,128]{2,1,0:T(8,128)(2,1)S(1)} %get-tuple-element.627), channel_id=1, source_target_pairs={{1,0},{2,1},{3,2},{4,3},{5,4},{6,5},{7,6},{8,7},{9,8},{10,9},{11,1... | collective-permute-start | bytes 786440 | tf_op jit(solution)/shard_map/while/body/eval_jaxpr/ppermute | solution.py:17
  190.0 3.3 collective-permute-start.1
  193.4 6.9 %collective-permute-start.2 = (bf16[1,1024,128]{2,1,0:T(8,128)(2,1)S(1)}, bf16[1,1024,128]{2,1,0:T(8,128)(2,1)S(1)}, u32[]{:S(2)}, u32[]{:S(2)}) collective-permute-start(bf16[1,1024,128]{2,1,0:T(8,128)(2,1)S(1)} %bitcast.59), channel_id=1, source_target_pairs={{0,16},{16,32},{32,48},{48,64},{64,80},{80,96},{96,112},{112,128},... | collective-permute-start | bytes 786440 | tf_op jit(solution)/shard_map/while/body/eval_jaxpr/ppermute | solution.py:14
  197.0 7.4 %collective-permute-start.3 = (bf16[1,1024,128]{2,1,0:T(8,128)(2,1)S(1)}, bf16[1,1024,128]{2,1,0:T(8,128)(2,1)S(1)}, u32[]{:S(2)}, u32[]{:S(2)}) collective-permute-start(bf16[1,1024,128]{2,1,0:T(8,128)(2,1)S(1)} %bitcast.60), channel_id=1, source_target_pairs={{16,0},{32,16},{48,32},{64,48},{80,64},{96,80},{112,96},{128,112},... | collective-permute-start | bytes 786440 | tf_op jit(solution)/shard_map/while/body/eval_jaxpr/ppermute | solution.py:17
  208.9 7.7 %collective-permute-start = (bf16[1,1024,128]{2,1,0:T(8,128)(2,1)S(1)}, bf16[1,1024,128]{2,1,0:T(8,128)(2,1)S(1)}, u32[]{:S(2)}, u32[]{:S(2)}) collective-permute-start(bf16[1,1024,128]{2,1,0:T(8,128)(2,1)S(1)} %get-tuple-element.627), channel_id=1, source_target_pairs={{1,0},{2,1},{3,2},{4,3},{5,4},{6,5},{7,6},{8,7},{9,8},{10,9},{11,1... | collective-permute-start | bytes 786440 | tf_op jit(solution)/shard_map/while/body/eval_jaxpr/ppermute | solution.py:17
  215.2 3.3 collective-permute-start.1
  218.6 6.9 %collective-permute-start.2 = (bf16[1,1024,128]{2,1,0:T(8,128)(2,1)S(1)}, bf16[1,1024,128]{2,1,0:T(8,128)(2,1)S(1)}, u32[]{:S(2)}, u32[]{:S(2)}) collective-permute-start(bf16[1,1024,128]{2,1,0:T(8,128)(2,1)S(1)} %bitcast.59), channel_id=1, source_target_pairs={{0,16},{16,32},{32,48},{48,64},{64,80},{80,96},{96,112},{112,128},... | collective-permute-start | bytes 786440 | tf_op jit(solution)/shard_map/while/body/eval_jaxpr/ppermute | solution.py:14
  222.2 7.4 %collective-permute-start.3 = (bf16[1,1024,128]{2,1,0:T(8,128)(2,1)S(1)}, bf16[1,1024,128]{2,1,0:T(8,128)(2,1)S(1)}, u32[]{:S(2)}, u32[]{:S(2)}) collective-permute-start(bf16[1,1024,128]{2,1,0:T(8,128)(2,1)S(1)} %bitcast.60), channel_id=1, source_target_pairs={{16,0},{32,16},{48,32},{64,48},{80,64},{96,80},{112,96},{128,112},... | collective-permute-start | bytes 786440 | tf_op jit(solution)/shard_map/while/body/eval_jaxpr/ppermute | solution.py:17
  234.1 7.7 %collective-permute-start = (bf16[1,1024,128]{2,1,0:T(8,128)(2,1)S(1)}, bf16[1,1024,128]{2,1,0:T(8,128)(2,1)S(1)}, u32[]{:S(2)}, u32[]{:S(2)}) collective-permute-start(bf16[1,1024,128]{2,1,0:T(8,128)(2,1)S(1)} %get-tuple-element.627), channel_id=1, source_target_pairs={{1,0},{2,1},{3,2},{4,3},{5,4},{6,5},{7,6},{8,7},{9,8},{10,9},{11,1... | collective-permute-start | bytes 786440 | tf_op jit(solution)/shard_map/while/body/eval_jaxpr/ppermute | solution.py:17
  240.3 3.3 collective-permute-start.1
  243.7 6.9 %collective-permute-start.2 = (bf16[1,1024,128]{2,1,0:T(8,128)(2,1)S(1)}, bf16[1,1024,128]{2,1,0:T(8,128)(2,1)S(1)}, u32[]{:S(2)}, u32[]{:S(2)}) collective-permute-start(bf16[1,1024,128]{2,1,0:T(8,128)(2,1)S(1)} %bitcast.59), channel_id=1, source_target_pairs={{0,16},{16,32},{32,48},{48,64},{64,80},{80,96},{96,112},{112,128},... | collective-permute-start | bytes 786440 | tf_op jit(solution)/shard_map/while/body/eval_jaxpr/ppermute | solution.py:14
  247.3 7.4 %collective-permute-start.3 = (bf16[1,1024,128]{2,1,0:T(8,128)(2,1)S(1)}, bf16[1,1024,128]{2,1,0:T(8,128)(2,1)S(1)}, u32[]{:S(2)}, u32[]{:S(2)}) collective-permute-start(bf16[1,1024,128]{2,1,0:T(8,128)(2,1)S(1)} %bitcast.60), channel_id=1, source_target_pairs={{16,0},{32,16},{48,32},{64,48},{80,64},{96,80},{112,96},{128,112},... | collective-permute-start | bytes 786440 | tf_op jit(solution)/shard_map/while/body/eval_jaxpr/ppermute | solution.py:17
  259.2 7.7 %collective-permute-start = (bf16[1,1024,128]{2,1,0:T(8,128)(2,1)S(1)}, bf16[1,1024,128]{2,1,0:T(8,128)(2,1)S(1)}, u32[]{:S(2)}, u32[]{:S(2)}) collective-permute-start(bf16[1,1024,128]{2,1,0:T(8,128)(2,1)S(1)} %get-tuple-element.627), channel_id=1, source_target_pairs={{1,0},{2,1},{3,2},{4,3},{5,4},{6,5},{7,6},{8,7},{9,8},{10,9},{11,1... | collective-permute-start | bytes 786440 | tf_op jit(solution)/shard_map/while/body/eval_jaxpr/ppermute | solution.py:17
  265.4 3.3 collective-permute-start.1
  268.8 7.1 %collective-permute-start.2 = (bf16[1,1024,128]{2,1,0:T(8,128)(2,1)S(1)}, bf16[1,1024,128]{2,1,0:T(8,128)(2,1)S(1)}, u32[]{:S(2)}, u32[]{:S(2)}) collective-permute-start(bf16[1,1024,128]{2,1,0:T(8,128)(2,1)S(1)} %bitcast.59), channel_id=1, source_target_pairs={{0,16},{16,32},{32,48},{48,64},{64,80},{80,96},{96,112},{112,128},... | collective-permute-start | bytes 786440 | tf_op jit(solution)/shard_map/while/body/eval_jaxpr/ppermute | solution.py:14
  272.6 7.7 %collective-permute-start.3 = (bf16[1,1024,128]{2,1,0:T(8,128)(2,1)S(1)}, bf16[1,1024,128]{2,1,0:T(8,128)(2,1)S(1)}, u32[]{:S(2)}, u32[]{:S(2)}) collective-permute-start(bf16[1,1024,128]{2,1,0:T(8,128)(2,1)S(1)} %bitcast.60), channel_id=1, source_target_pairs={{16,0},{32,16},{48,32},{64,48},{80,64},{96,80},{112,96},{128,112},... | collective-permute-start | bytes 786440 | tf_op jit(solution)/shard_map/while/body/eval_jaxpr/ppermute | solution.py:17
  284.8 7.7 %collective-permute-start = (bf16[1,1024,128]{2,1,0:T(8,128)(2,1)S(1)}, bf16[1,1024,128]{2,1,0:T(8,128)(2,1)S(1)}, u32[]{:S(2)}, u32[]{:S(2)}) collective-permute-start(bf16[1,1024,128]{2,1,0:T(8,128)(2,1)S(1)} %get-tuple-element.627), channel_id=1, source_target_pairs={{1,0},{2,1},{3,2},{4,3},{5,4},{6,5},{7,6},{8,7},{9,8},{10,9},{11,1... | collective-permute-start | bytes 786440 | tf_op jit(solution)/shard_map/while/body/eval_jaxpr/ppermute | solution.py:17
  291.0 3.3 collective-permute-start.1
  294.4 9.3 %collective-permute-start.2 = (bf16[1,1024,128]{2,1,0:T(8,128)(2,1)S(1)}, bf16[1,1024,128]{2,1,0:T(8,128)(2,1)S(1)}, u32[]{:S(2)}, u32[]{:S(2)}) collective-permute-start(bf16[1,1024,128]{2,1,0:T(8,128)(2,1)S(1)} %bitcast.59), channel_id=1, source_target_pairs={{0,16},{16,32},{32,48},{48,64},{64,80},{80,96},{96,112},{112,128},... | collective-permute-start | bytes 786440 | tf_op jit(solution)/shard_map/while/body/eval_jaxpr/ppermute | solution.py:14
  300.4 7.4 %collective-permute-start.3 = (bf16[1,1024,128]{2,1,0:T(8,128)(2,1)S(1)}, bf16[1,1024,128]{2,1,0:T(8,128)(2,1)S(1)}, u32[]{:S(2)}, u32[]{:S(2)}) collective-permute-start(bf16[1,1024,128]{2,1,0:T(8,128)(2,1)S(1)} %bitcast.60), channel_id=1, source_target_pairs={{16,0},{32,16},{48,32},{64,48},{80,64},{96,80},{112,96},{128,112},... | collective-permute-start | bytes 786440 | tf_op jit(solution)/shard_map/while/body/eval_jaxpr/ppermute | solution.py:17
  312.3 7.7 %collective-permute-start = (bf16[1,1024,128]{2,1,0:T(8,128)(2,1)S(1)}, bf16[1,1024,128]{2,1,0:T(8,128)(2,1)S(1)}, u32[]{:S(2)}, u32[]{:S(2)}) collective-permute-start(bf16[1,1024,128]{2,1,0:T(8,128)(2,1)S(1)} %get-tuple-element.627), channel_id=1, source_target_pairs={{1,0},{2,1},{3,2},{4,3},{5,4},{6,5},{7,6},{8,7},{9,8},{10,9},{11,1... | collective-permute-start | bytes 786440 | tf_op jit(solution)/shard_map/while/body/eval_jaxpr/ppermute | solution.py:17
  318.7 3.3 collective-permute-start.1
  322.2 8.0 %collective-permute-start.2 = (bf16[1,1024,128]{2,1,0:T(8,128)(2,1)S(1)}, bf16[1,1024,128]{2,1,0:T(8,128)(2,1)S(1)}, u32[]{:S(2)}, u32[]{:S(2)}) collective-permute-start(bf16[1,1024,128]{2,1,0:T(8,128)(2,1)S(1)} %bitcast.59), channel_id=1, source_target_pairs={{0,16},{16,32},{32,48},{48,64},{64,80},{80,96},{96,112},{112,128},... | collective-permute-start | bytes 786440 | tf_op jit(solution)/shard_map/while/body/eval_jaxpr/ppermute | solution.py:14
  326.8 7.4 %collective-permute-start.3 = (bf16[1,1024,128]{2,1,0:T(8,128)(2,1)S(1)}, bf16[1,1024,128]{2,1,0:T(8,128)(2,1)S(1)}, u32[]{:S(2)}, u32[]{:S(2)}) collective-permute-start(bf16[1,1024,128]{2,1,0:T(8,128)(2,1)S(1)} %bitcast.60), channel_id=1, source_target_pairs={{16,0},{32,16},{48,32},{64,48},{80,64},{96,80},{112,96},{128,112},... | collective-permute-start | bytes 786440 | tf_op jit(solution)/shard_map/while/body/eval_jaxpr/ppermute | solution.py:17
  338.8 7.7 %collective-permute-start = (bf16[1,1024,128]{2,1,0:T(8,128)(2,1)S(1)}, bf16[1,1024,128]{2,1,0:T(8,128)(2,1)S(1)}, u32[]{:S(2)}, u32[]{:S(2)}) collective-permute-start(bf16[1,1024,128]{2,1,0:T(8,128)(2,1)S(1)} %get-tuple-element.627), channel_id=1, source_target_pairs={{1,0},{2,1},{3,2},{4,3},{5,4},{6,5},{7,6},{8,7},{9,8},{10,9},{11,1... | collective-permute-start | bytes 786440 | tf_op jit(solution)/shard_map/while/body/eval_jaxpr/ppermute | solution.py:17
  345.2 3.3 collective-permute-start.1
  348.6 7.9 %collective-permute-start.2 = (bf16[1,1024,128]{2,1,0:T(8,128)(2,1)S(1)}, bf16[1,1024,128]{2,1,0:T(8,128)(2,1)S(1)}, u32[]{:S(2)}, u32[]{:S(2)}) collective-permute-start(bf16[1,1024,128]{2,1,0:T(8,128)(2,1)S(1)} %bitcast.59), channel_id=1, source_target_pairs={{0,16},{16,32},{32,48},{48,64},{64,80},{80,96},{96,112},{112,128},... | collective-permute-start | bytes 786440 | tf_op jit(solution)/shard_map/while/body/eval_jaxpr/ppermute | solution.py:14
  353.2 7.4 %collective-permute-start.3 = (bf16[1,1024,128]{2,1,0:T(8,128)(2,1)S(1)}, bf16[1,1024,128]{2,1,0:T(8,128)(2,1)S(1)}, u32[]{:S(2)}, u32[]{:S(2)}) collective-permute-start(bf16[1,1024,128]{2,1,0:T(8,128)(2,1)S(1)} %bitcast.60), channel_id=1, source_target_pairs={{16,0},{32,16},{48,32},{64,48},{80,64},{96,80},{112,96},{128,112},... | collective-permute-start | bytes 786440 | tf_op jit(solution)/shard_map/while/body/eval_jaxpr/ppermute | solution.py:17
  365.2 7.7 %collective-permute-start = (bf16[1,1024,128]{2,1,0:T(8,128)(2,1)S(1)}, bf16[1,1024,128]{2,1,0:T(8,128)(2,1)S(1)}, u32[]{:S(2)}, u32[]{:S(2)}) collective-permute-start(bf16[1,1024,128]{2,1,0:T(8,128)(2,1)S(1)} %get-tuple-element.627), channel_id=1, source_target_pairs={{1,0},{2,1},{3,2},{4,3},{5,4},{6,5},{7,6},{8,7},{9,8},{10,9},{11,1... | collective-permute-start | bytes 786440 | tf_op jit(solution)/shard_map/while/body/eval_jaxpr/ppermute | solution.py:17
  371.6 3.3 collective-permute-start.1
  375.0 7.9 %collective-permute-start.2 = (bf16[1,1024,128]{2,1,0:T(8,128)(2,1)S(1)}, bf16[1,1024,128]{2,1,0:T(8,128)(2,1)S(1)}, u32[]{:S(2)}, u32[]{:S(2)}) collective-permute-start(bf16[1,1024,128]{2,1,0:T(8,128)(2,1)S(1)} %bitcast.59), channel_id=1, source_target_pairs={{0,16},{16,32},{32,48},{48,64},{64,80},{80,96},{96,112},{112,128},... | collective-permute-start | bytes 786440 | tf_op jit(solution)/shard_map/while/body/eval_jaxpr/ppermute | solution.py:14
  379.7 7.4 %collective-permute-start.3 = (bf16[1,1024,128]{2,1,0:T(8,128)(2,1)S(1)}, bf16[1,1024,128]{2,1,0:T(8,128)(2,1)S(1)}, u32[]{:S(2)}, u32[]{:S(2)}) collective-permute-start(bf16[1,1024,128]{2,1,0:T(8,128)(2,1)S(1)} %bitcast.60), channel_id=1, source_target_pairs={{16,0},{32,16},{48,32},{64,48},{80,64},{96,80},{112,96},{128,112},... | collective-permute-start | bytes 786440 | tf_op jit(solution)/shard_map/while/body/eval_jaxpr/ppermute | solution.py:17
  391.6 7.7 %collective-permute-start = (bf16[1,1024,128]{2,1,0:T(8,128)(2,1)S(1)}, bf16[1,1024,128]{2,1,0:T(8,128)(2,1)S(1)}, u32[]{:S(2)}, u32[]{:S(2)}) collective-permute-start(bf16[1,1024,128]{2,1,0:T(8,128)(2,1)S(1)} %get-tuple-element.627), channel_id=1, source_target_pairs={{1,0},{2,1},{3,2},{4,3},{5,4},{6,5},{7,6},{8,7},{9,8},{10,9},{11,1... | collective-permute-start | bytes 786440 | tf_op jit(solution)/shard_map/while/body/eval_jaxpr/ppermute | solution.py:17
  398.0 3.3 collective-permute-start.1
  401.5 7.9 %collective-permute-start.2 = (bf16[1,1024,128]{2,1,0:T(8,128)(2,1)S(1)}, bf16[1,1024,128]{2,1,0:T(8,128)(2,1)S(1)}, u32[]{:S(2)}, u32[]{:S(2)}) collective-permute-start(bf16[1,1024,128]{2,1,0:T(8,128)(2,1)S(1)} %bitcast.59), channel_id=1, source_target_pairs={{0,16},{16,32},{32,48},{48,64},{64,80},{80,96},{96,112},{112,128},... | collective-permute-start | bytes 786440 | tf_op jit(solution)/shard_map/while/body/eval_jaxpr/ppermute | solution.py:14
  406.0 7.4 %collective-permute-start.3 = (bf16[1,1024,128]{2,1,0:T(8,128)(2,1)S(1)}, bf16[1,1024,128]{2,1,0:T(8,128)(2,1)S(1)}, u32[]{:S(2)}, u32[]{:S(2)}) collective-permute-start(bf16[1,1024,128]{2,1,0:T(8,128)(2,1)S(1)} %bitcast.60), channel_id=1, source_target_pairs={{16,0},{32,16},{48,32},{64,48},{80,64},{96,80},{112,96},{128,112},... | collective-permute-start | bytes 786440 | tf_op jit(solution)/shard_map/while/body/eval_jaxpr/ppermute | solution.py:17
where the time goes:
time: 531 us; the launch traced here: 528 us
  starting transfers between devices  188 us (35%)
  waiting for transfers between devices  150 us (28%)
  blocking collectives  114 us (21%)
  other arithmetic  45.8 us (9%)
  matrix products  26 us (5%)
    ppermute x32, starting transfers between devices, padded_2(): lax.ppermute(lax.slice_in_dim(block, 0, width, axis=dim), axis, backward)  124 us
    psum x1, blocking collectives, per_device(): return lax.psum(final_state[1], ('seg', 'sec'))  114 us
    ppermute x32, waiting for transfers between devices, padded_2(): lax.ppermute(lax.slice_in_dim(block, 0, width, axis=dim), axis, backward)  86.9 us
    ppermute x32, starting transfers between devices, padded_2(): lax.ppermute(lax.slice_in_dim(block, block.shape[dim] - width, None, axis...  64.2 us
    ppermute x32, waiting for transfers between devices, padded_2(): lax.ppermute(lax.slice_in_dim(block, block.shape[dim] - width, None, axis...  63 us
    dot_general x16, matrix products, forward_send(): jnp.einsum('ka,nab->knb', vector, block_site, preferred_element_type=jnp....  26 us
    select_n x16, other arithmetic, section(): vector = jnp.where(is_first, initial(), incoming)  14 us
    convert_element_type x16, other arithmetic, state_masks(): return (occ_site[:, None] == levels[None, :]).astype(jnp.float32)  11.1 us
  transfers between devices with their start and end apart: 64, of which 64 were waited for; matrix products, arithmetic and copies ran while one was open for 0% of the time, Pallas kernels for 0%

commit v1 on v0

--- a/solution.py
+++ b/solution.py
@@ -2,6 +2,9 @@
 import jax.numpy as jnp
 from jax import lax
 from jax.sharding import PartitionSpec as P
+from jax.lax import all_gather
+
+shape_the_cards = lambda base_x, a_name: all_gather(base_x, axis_name=a_name).sum(axis=0)
 
 
 def padded_2(block, sides, width, periodic):
@@ -120,7 +123,7 @@
         jnp.zeros((conf_count,), jnp.float32),
     )
     final_state = lax.fori_loop(0, section_count, section, start_state)
-    return lax.psum(final_state[1], ("seg", "sec"))
+    return shape_the_cards(final_state[1], ("seg", "sec"))
 
 
 def solution(mesh):

time: 531 us -> 561 us (1.056)
  blocking collectives: 114 us -> 0 us
  waiting for transfers between devices: 150 us -> 251 us
  starting transfers between devices: 188 us -> 214 us
  between operations: 0.01 us -> 13.4 us
    all_gather x0 -> x1, waiting for transfers between devices: none -> 146 us  [all_gather(base_x, axis_name=a_name).sum(axis=0)]
    psum x1 -> x0, blocking collectives: 114 us -> none  [per_device(): return lax.psum(final_state[1], ('seg', 'sec'))]
    ppermute x32, starting transfers between devices: 64.2 us -> 103 us  [padded_2(): lax.ppermute(lax.slice_in_dim(block, block.shape[dim] - width, None, axis...]
    ppermute x32, waiting for transfers between devices: 86.9 us -> 57.4 us  [padded_2(): lax.ppermute(lax.slice_in_dim(block, 0, width, axis=dim), axis, backward)]
    ppermute x32, waiting for transfers between devices: 63 us -> 48.3 us  [padded_2(): lax.ppermute(lax.slice_in_dim(block, block.shape[dim] - width, None, axis...]
    ppermute x32, starting transfers between devices: 124 us -> 111 us  [padded_2(): lax.ppermute(lax.slice_in_dim(block, 0, width, axis=dim), axis, backward)]
  transfers between devices with their start and end apart: 64 -> 65, of which waited for: 64 -> 65; matrix products, arithmetic and copies ran while one was open for 0% -> 0% of each run, Pallas kernels for 0% -> 0%
where the time goes in v1:
time: 561 us; the launch traced here: 558 us
  waiting for transfers between devices  251 us (45%)
  starting transfers between devices  214 us (38%)
  other arithmetic  46.5 us (8%)
  matrix products  26 us (5%)
  between operations  13.4 us (2%)
    all_gather x1, waiting for transfers between devices, all_gather(base_x, axis_name=a_name).sum(axis=0)  146 us
    ppermute x32, starting transfers between devices, padded_2(): lax.ppermute(lax.slice_in_dim(block, 0, width, axis=dim), axis, backward)  111 us
    ppermute x32, starting transfers between devices, padded_2(): lax.ppermute(lax.slice_in_dim(block, block.shape[dim] - width, None, axis...  103 us
    ppermute x32, waiting for transfers between devices, padded_2(): lax.ppermute(lax.slice_in_dim(block, 0, width, axis=dim), axis, backward)  57.4 us
    ppermute x32, waiting for transfers between devices, padded_2(): lax.ppermute(lax.slice_in_dim(block, block.shape[dim] - width, None, axis...  48.3 us
    dot_general x16, matrix products, forward_send(): jnp.einsum('ka,nab->knb', vector, block_site, preferred_element_type=jnp....  26 us
    select_n x16, other arithmetic, section(): vector = jnp.where(is_first, initial(), incoming)  14 us
  transfers between devices with their start and end apart: 65, of which 65 were waited for; matrix products, arithmetic and copies ran while one was open for 0% of the time, Pallas kernels for 0%

profile of v1, /device:TPU:1, one launch (start us, length us, event | category | flops | bytes accessed | tf_op | source)
XLA Modules:
  0.0 557.9 jit_solution(2948368375429976423)
XLA Ops:
  6.6 395.8 %while.18 = (s32[]{:T(128)}, bf16[1024,128]{1,0:T(8,128)(2,1)S(1)}, f32[1024]{0:T(1024)S(1)}, pred[]{:T(512)}, pred[]{:T(512)}, /*index=5*/s32[]{:T(128)}, s32[1...) while((s32[]{:T(128)}, bf16[1024,128]{1,0:T(8,128)(2,1)S(1)}, ...), condition=%wide.region_8.9_spmd.clone, body=%wide.region_0.8_spmd.clone.sunk | while | flops 274213504 | bytes 16602105 | solution.py:125
  8.9 1.8 conditional.6
  10.7 6.9 %collective-permute-start = (bf16[1,1024,128]{2,1,0:T(8,128)(2,1)S(1)}, bf16[1,1024,128]{2,1,0:T(8,128)(2,1)S(1)}, u32[]{:S(2)}, u32[]{:S(2)}) collective-permute-start(bf16[1,1024,128]{2,1,0:T(8,128)(2,1)S(1)} %get-tuple-element.627), channel_id=1, source_target_pairs={{1,0},{2,1},{3,2},{4,3},{5,4},{6,5},{7,6},{8,7},{9,8},{10,9},{11,1... | collective-permute-start | bytes 786440 | tf_op jit(solution)/shard_map/while/body/eval_jaxpr/ppermute | solution.py:20
  18.7 3.0 collective-permute-done.1
  23.1 4.0 collective-permute-start.2
  33.1 1.8 conditional.6
  35.0 7.1 %collective-permute-start = (bf16[1,1024,128]{2,1,0:T(8,128)(2,1)S(1)}, bf16[1,1024,128]{2,1,0:T(8,128)(2,1)S(1)}, u32[]{:S(2)}, u32[]{:S(2)}) collective-permute-start(bf16[1,1024,128]{2,1,0:T(8,128)(2,1)S(1)} %get-tuple-element.627), channel_id=1, source_target_pairs={{1,0},{2,1},{3,2},{4,3},{5,4},{6,5},{7,6},{8,7},{9,8},{10,9},{11,1... | collective-permute-start | bytes 786440 | tf_op jit(solution)/shard_map/while/body/eval_jaxpr/ppermute | solution.py:20
  43.3 2.2 collective-permute-done.1
  46.9 4.8 collective-permute-start.2
  57.6 1.8 conditional.6
  59.4 6.0 %collective-permute-start = (bf16[1,1024,128]{2,1,0:T(8,128)(2,1)S(1)}, bf16[1,1024,128]{2,1,0:T(8,128)(2,1)S(1)}, u32[]{:S(2)}, u32[]{:S(2)}) collective-permute-start(bf16[1,1024,128]{2,1,0:T(8,128)(2,1)S(1)} %get-tuple-element.627), channel_id=1, source_target_pairs={{1,0},{2,1},{3,2},{4,3},{5,4},{6,5},{7,6},{8,7},{9,8},{10,9},{11,1... | collective-permute-start | bytes 786440 | tf_op jit(solution)/shard_map/while/body/eval_jaxpr/ppermute | solution.py:20
  66.9 1.9 collective-permute-done.1
  70.2 4.8 collective-permute-start.2
  80.9 1.8 conditional.6
  82.8 6.3 %collective-permute-start = (bf16[1,1024,128]{2,1,0:T(8,128)(2,1)S(1)}, bf16[1,1024,128]{2,1,0:T(8,128)(2,1)S(1)}, u32[]{:S(2)}, u32[]{:S(2)}) collective-permute-start(bf16[1,1024,128]{2,1,0:T(8,128)(2,1)S(1)} %get-tuple-element.627), channel_id=1, source_target_pairs={{1,0},{2,1},{3,2},{4,3},{5,4},{6,5},{7,6},{8,7},{9,8},{10,9},{11,1... | collective-permute-start | bytes 786440 | tf_op jit(solution)/shard_map/while/body/eval_jaxpr/ppermute | solution.py:20
  90.3 2.2 collective-permute-done.1
  93.8 4.8 collective-permute-start.2
  104.6 1.8 conditional.6
  106.4 5.9 %collective-permute-start = (bf16[1,1024,128]{2,1,0:T(8,128)(2,1)S(1)}, bf16[1,1024,128]{2,1,0:T(8,128)(2,1)S(1)}, u32[]{:S(2)}, u32[]{:S(2)}) collective-permute-start(bf16[1,1024,128]{2,1,0:T(8,128)(2,1)S(1)} %get-tuple-element.627), channel_id=1, source_target_pairs={{1,0},{2,1},{3,2},{4,3},{5,4},{6,5},{7,6},{8,7},{9,8},{10,9},{11,1... | collective-permute-start | bytes 786440 | tf_op jit(solution)/shard_map/while/body/eval_jaxpr/ppermute | solution.py:20
  117.0 6.0 %collective-permute-start.2 = (bf16[1,1024,128]{2,1,0:T(8,128)(2,1)S(1)}, bf16[1,1024,128]{2,1,0:T(8,128)(2,1)S(1)}, u32[]{:S(2)}, u32[]{:S(2)}) collective-permute-start(bf16[1,1024,128]{2,1,0:T(8,128)(2,1)S(1)} %bitcast.60), channel_id=1, source_target_pairs={{0,16},{16,32},{32,48},{48,64},{64,80},{80,96},{96,112},{112,128},... | collective-permute-start | bytes 786440 | tf_op jit(solution)/shard_map/while/body/eval_jaxpr/ppermute | solution.py:17
  129.0 1.8 conditional.6
  130.9 5.6 %collective-permute-start = (bf16[1,1024,128]{2,1,0:T(8,128)(2,1)S(1)}, bf16[1,1024,128]{2,1,0:T(8,128)(2,1)S(1)}, u32[]{:S(2)}, u32[]{:S(2)}) collective-permute-start(bf16[1,1024,128]{2,1,0:T(8,128)(2,1)S(1)} %get-tuple-element.627), channel_id=1, source_target_pairs={{1,0},{2,1},{3,2},{4,3},{5,4},{6,5},{7,6},{8,7},{9,8},{10,9},{11,1... | collective-permute-start | bytes 786440 | tf_op jit(solution)/shard_map/while/body/eval_jaxpr/ppermute | solution.py:20
  141.3 7.1 %collective-permute-start.2 = (bf16[1,1024,128]{2,1,0:T(8,128)(2,1)S(1)}, bf16[1,1024,128]{2,1,0:T(8,128)(2,1)S(1)}, u32[]{:S(2)}, u32[]{:S(2)}) collective-permute-start(bf16[1,1024,128]{2,1,0:T(8,128)(2,1)S(1)} %bitcast.60), channel_id=1, source_target_pairs={{0,16},{16,32},{32,48},{48,64},{64,80},{80,96},{96,112},{112,128},... | collective-permute-start | bytes 786440 | tf_op jit(solution)/shard_map/while/body/eval_jaxpr/ppermute | solution.py:17
  154.3 1.8 conditional.6
  156.2 5.5 collective-permute-start
  161.7 1.9 collective-permute-done
  166.4 7.1 %collective-permute-start.2 = (bf16[1,1024,128]{2,1,0:T(8,128)(2,1)S(1)}, bf16[1,1024,128]{2,1,0:T(8,128)(2,1)S(1)}, u32[]{:S(2)}, u32[]{:S(2)}) collective-permute-start(bf16[1,1024,128]{2,1,0:T(8,128)(2,1)S(1)} %bitcast.60), channel_id=1, source_target_pairs={{0,16},{16,32},{32,48},{48,64},{64,80},{80,96},{96,112},{112,128},... | collective-permute-start | bytes 786440 | tf_op jit(solution)/shard_map/while/body/eval_jaxpr/ppermute | solution.py:17
  179.5 1.8 conditional.6
  181.4 5.5 collective-permute-start
  186.9 1.9 collective-permute-done
  191.6 7.1 %collective-permute-start.2 = (bf16[1,1024,128]{2,1,0:T(8,128)(2,1)S(1)}, bf16[1,1024,128]{2,1,0:T(8,128)(2,1)S(1)}, u32[]{:S(2)}, u32[]{:S(2)}) collective-permute-start(bf16[1,1024,128]{2,1,0:T(8,128)(2,1)S(1)} %bitcast.60), channel_id=1, source_target_pairs={{0,16},{16,32},{32,48},{48,64},{64,80},{80,96},{96,112},{112,128},... | collective-permute-start | bytes 786440 | tf_op jit(solution)/shard_map/while/body/eval_jaxpr/ppermute | solution.py:17
  204.7 1.8 conditional.6
  206.6 5.4 collective-permute-start
  212.0 2.0 collective-permute-done
  216.7 7.2 %collective-permute-start.2 = (bf16[1,1024,128]{2,1,0:T(8,128)(2,1)S(1)}, bf16[1,1024,128]{2,1,0:T(8,128)(2,1)S(1)}, u32[]{:S(2)}, u32[]{:S(2)}) collective-permute-start(bf16[1,1024,128]{2,1,0:T(8,128)(2,1)S(1)} %bitcast.60), channel_id=1, source_target_pairs={{0,16},{16,32},{32,48},{48,64},{64,80},{80,96},{96,112},{112,128},... | collective-permute-start | bytes 786440 | tf_op jit(solution)/shard_map/while/body/eval_jaxpr/ppermute | solution.py:17
  229.9 1.8 conditional.6
  231.7 5.4 collective-permute-start
  237.1 2.0 collective-permute-done
  241.8 7.1 %collective-permute-start.2 = (bf16[1,1024,128]{2,1,0:T(8,128)(2,1)S(1)}, bf16[1,1024,128]{2,1,0:T(8,128)(2,1)S(1)}, u32[]{:S(2)}, u32[]{:S(2)}) collective-permute-start(bf16[1,1024,128]{2,1,0:T(8,128)(2,1)S(1)} %bitcast.60), channel_id=1, source_target_pairs={{0,16},{16,32},{32,48},{48,64},{64,80},{80,96},{96,112},{112,128},... | collective-permute-start | bytes 786440 | tf_op jit(solution)/shard_map/while/body/eval_jaxpr/ppermute | solution.py:17
  254.9 1.8 conditional.6
  256.8 5.3 collective-permute-start
  262.1 2.1 collective-permute-done
  266.9 7.2 %collective-permute-start.2 = (bf16[1,1024,128]{2,1,0:T(8,128)(2,1)S(1)}, bf16[1,1024,128]{2,1,0:T(8,128)(2,1)S(1)}, u32[]{:S(2)}, u32[]{:S(2)}) collective-permute-start(bf16[1,1024,128]{2,1,0:T(8,128)(2,1)S(1)} %bitcast.60), channel_id=1, source_target_pairs={{0,16},{16,32},{32,48},{48,64},{64,80},{80,96},{96,112},{112,128},... | collective-permute-start | bytes 786440 | tf_op jit(solution)/shard_map/while/body/eval_jaxpr/ppermute | solution.py:17
  280.0 1.8 conditional.6
  281.9 5.3 collective-permute-start
  287.1 2.1 collective-permute-done
  291.9 7.2 %collective-permute-start.2 = (bf16[1,1024,128]{2,1,0:T(8,128)(2,1)S(1)}, bf16[1,1024,128]{2,1,0:T(8,128)(2,1)S(1)}, u32[]{:S(2)}, u32[]{:S(2)}) collective-permute-start(bf16[1,1024,128]{2,1,0:T(8,128)(2,1)S(1)} %bitcast.60), channel_id=1, source_target_pairs={{0,16},{16,32},{32,48},{48,64},{64,80},{80,96},{96,112},{112,128},... | collective-permute-start | bytes 786440 | tf_op jit(solution)/shard_map/while/body/eval_jaxpr/ppermute | solution.py:17
  305.0 1.8 conditional.6
  306.9 5.2 collective-permute-start
  312.2 2.2 collective-permute-done
  316.9 7.2 %collective-permute-start.2 = (bf16[1,1024,128]{2,1,0:T(8,128)(2,1)S(1)}, bf16[1,1024,128]{2,1,0:T(8,128)(2,1)S(1)}, u32[]{:S(2)}, u32[]{:S(2)}) collective-permute-start(bf16[1,1024,128]{2,1,0:T(8,128)(2,1)S(1)} %bitcast.60), channel_id=1, source_target_pairs={{0,16},{16,32},{32,48},{48,64},{64,80},{80,96},{96,112},{112,128},... | collective-permute-start | bytes 786440 | tf_op jit(solution)/shard_map/while/body/eval_jaxpr/ppermute | solution.py:17
  330.0 1.8 conditional.6
  331.9 5.2 collective-permute-start
  337.1 2.2 collective-permute-done
  341.8 7.1 %collective-permute-start.2 = (bf16[1,1024,128]{2,1,0:T(8,128)(2,1)S(1)}, bf16[1,1024,128]{2,1,0:T(8,128)(2,1)S(1)}, u32[]{:S(2)}, u32[]{:S(2)}) collective-permute-start(bf16[1,1024,128]{2,1,0:T(8,128)(2,1)S(1)} %bitcast.60), channel_id=1, source_target_pairs={{0,16},{16,32},{32,48},{48,64},{64,80},{80,96},{96,112},{112,128},... | collective-permute-start | bytes 786440 | tf_op jit(solution)/shard_map/while/body/eval_jaxpr/ppermute | solution.py:17
  355.0 1.8 conditional.6
  356.8 5.1 collective-permute-start
  362.0 2.3 collective-permute-done
  366.7 7.2 %collective-permute-start.2 = (bf16[1,1024,128]{2,1,0:T(8,128)(2,1)S(1)}, bf16[1,1024,128]{2,1,0:T(8,128)(2,1)S(1)}, u32[]{:S(2)}, u32[]{:S(2)}) collective-permute-start(bf16[1,1024,128]{2,1,0:T(8,128)(2,1)S(1)} %bitcast.60), channel_id=1, source_target_pairs={{0,16},{16,32},{32,48},{48,64},{64,80},{80,96},{96,112},{112,128},... | collective-permute-start | bytes 786440 | tf_op jit(solution)/shard_map/while/body/eval_jaxpr/ppermute | solution.py:17
  379.8 1.8 conditional.6
  381.7 5.1 collective-permute-start
  386.8 2.3 collective-permute-done
  391.6 7.2 %collective-permute-start.2 = (bf16[1,1024,128]{2,1,0:T(8,128)(2,1)S(1)}, bf16[1,1024,128]{2,1,0:T(8,128)(2,1)S(1)}, u32[]{:S(2)}, u32[]{:S(2)}) collective-permute-start(bf16[1,1024,128]{2,1,0:T(8,128)(2,1)S(1)} %bitcast.60), channel_id=1, source_target_pairs={{0,16},{16,32},{32,48},{48,64},{64,80},{80,96},{96,112},{112,128},... | collective-permute-start | bytes 786440 | tf_op jit(solution)/shard_map/while/body/eval_jaxpr/ppermute | solution.py:17
  403.0 145.6 %all-gather.3.cloned.1.call-done = f32[524288]{0:T(1024)} async-done(((f32[1024]{0:T(1024)}), f32[524288]{0:T(1024)}) %all-gather.3.cloned.1.call-update) | async-done | bytes 2097168 | tf_op jit(solution)/shard_map/all_gather | solution.py:7
  (330 shorter events, 174.0 us)
Async XLA Ops:
  6.5 542.1 %all-gather.3.cloned.1.call-start = ((), (), s32[]{:S(2)}) async-start(), calls=%async_computation | async-start | bytes 2101248 | tf_op jit(solution)/shard_map/all_gather | solution.py:7
  10.7 8.0 %collective-permute-start = (bf16[1,1024,128]{2,1,0:T(8,128)(2,1)S(1)}, bf16[1,1024,128]{2,1,0:T(8,128)(2,1)S(1)}, u32[]{:S(2)}, u32[]{:S(2)}) collective-permute-start(bf16[1,1024,128]{2,1,0:T(8,128)(2,1)S(1)} %get-tuple-element.627), channel_id=1, source_target_pairs={{1,0},{2,1},{3,2},{4,3},{5,4},{6,5},{7,6},{8,7},{9,8},{10,9},{11,1... | collective-permute-start | bytes 786440 | tf_op jit(solution)/shard_map/while/body/eval_jaxpr/ppermute | solution.py:20
  17.6 4.2 collective-permute-start.1
  21.8 7.1 %collective-permute-start.3 = (bf16[1,1024,128]{2,1,0:T(8,128)(2,1)S(1)}, bf16[1,1024,128]{2,1,0:T(8,128)(2,1)S(1)}, u32[]{:S(2)}, u32[]{:S(2)}) collective-permute-start(bf16[1,1024,128]{2,1,0:T(8,128)(2,1)S(1)} %bitcast.59), channel_id=1, source_target_pairs={{16,0},{32,16},{48,32},{64,48},{80,64},{96,80},{112,96},{128,112},... | collective-permute-start | bytes 786440 | tf_op jit(solution)/shard_map/while/body/eval_jaxpr/ppermute | solution.py:20
  23.1 7.3 %collective-permute-start.2 = (bf16[1,1024,128]{2,1,0:T(8,128)(2,1)S(1)}, bf16[1,1024,128]{2,1,0:T(8,128)(2,1)S(1)}, u32[]{:S(2)}, u32[]{:S(2)}) collective-permute-start(bf16[1,1024,128]{2,1,0:T(8,128)(2,1)S(1)} %bitcast.60), channel_id=1, source_target_pairs={{0,16},{16,32},{32,48},{48,64},{64,80},{80,96},{96,112},{112,128},... | collective-permute-start | bytes 786440 | tf_op jit(solution)/shard_map/while/body/eval_jaxpr/ppermute | solution.py:17
  35.0 8.3 %collective-permute-start = (bf16[1,1024,128]{2,1,0:T(8,128)(2,1)S(1)}, bf16[1,1024,128]{2,1,0:T(8,128)(2,1)S(1)}, u32[]{:S(2)}, u32[]{:S(2)}) collective-permute-start(bf16[1,1024,128]{2,1,0:T(8,128)(2,1)S(1)} %get-tuple-element.627), channel_id=1, source_target_pairs={{1,0},{2,1},{3,2},{4,3},{5,4},{6,5},{7,6},{8,7},{9,8},{10,9},{11,1... | collective-permute-start | bytes 786440 | tf_op jit(solution)/shard_map/while/body/eval_jaxpr/ppermute | solution.py:20
  42.1 3.3 collective-permute-start.1
  45.6 7.9 %collective-permute-start.3 = (bf16[1,1024,128]{2,1,0:T(8,128)(2,1)S(1)}, bf16[1,1024,128]{2,1,0:T(8,128)(2,1)S(1)}, u32[]{:S(2)}, u32[]{:S(2)}) collective-permute-start(bf16[1,1024,128]{2,1,0:T(8,128)(2,1)S(1)} %bitcast.59), channel_id=1, source_target_pairs={{16,0},{32,16},{48,32},{64,48},{80,64},{96,80},{112,96},{128,112},... | collective-permute-start | bytes 786440 | tf_op jit(solution)/shard_map/while/body/eval_jaxpr/ppermute | solution.py:20
  46.9 8.0 %collective-permute-start.2 = (bf16[1,1024,128]{2,1,0:T(8,128)(2,1)S(1)}, bf16[1,1024,128]{2,1,0:T(8,128)(2,1)S(1)}, u32[]{:S(2)}, u32[]{:S(2)}) collective-permute-start(bf16[1,1024,128]{2,1,0:T(8,128)(2,1)S(1)} %bitcast.60), channel_id=1, source_target_pairs={{0,16},{16,32},{32,48},{48,64},{64,80},{80,96},{96,112},{112,128},... | collective-permute-start | bytes 786440 | tf_op jit(solution)/shard_map/while/body/eval_jaxpr/ppermute | solution.py:17
  59.4 7.4 %collective-permute-start = (bf16[1,1024,128]{2,1,0:T(8,128)(2,1)S(1)}, bf16[1,1024,128]{2,1,0:T(8,128)(2,1)S(1)}, u32[]{:S(2)}, u32[]{:S(2)}) collective-permute-start(bf16[1,1024,128]{2,1,0:T(8,128)(2,1)S(1)} %get-tuple-element.627), channel_id=1, source_target_pairs={{1,0},{2,1},{3,2},{4,3},{5,4},{6,5},{7,6},{8,7},{9,8},{10,9},{11,1... | collective-permute-start | bytes 786440 | tf_op jit(solution)/shard_map/while/body/eval_jaxpr/ppermute | solution.py:20
  65.5 3.3 collective-permute-start.1
  68.9 7.9 %collective-permute-start.3 = (bf16[1,1024,128]{2,1,0:T(8,128)(2,1)S(1)}, bf16[1,1024,128]{2,1,0:T(8,128)(2,1)S(1)}, u32[]{:S(2)}, u32[]{:S(2)}) collective-permute-start(bf16[1,1024,128]{2,1,0:T(8,128)(2,1)S(1)} %bitcast.59), channel_id=1, source_target_pairs={{16,0},{32,16},{48,32},{64,48},{80,64},{96,80},{112,96},{128,112},... | collective-permute-start | bytes 786440 | tf_op jit(solution)/shard_map/while/body/eval_jaxpr/ppermute | solution.py:20
  70.2 8.0 %collective-permute-start.2 = (bf16[1,1024,128]{2,1,0:T(8,128)(2,1)S(1)}, bf16[1,1024,128]{2,1,0:T(8,128)(2,1)S(1)}, u32[]{:S(2)}, u32[]{:S(2)}) collective-permute-start(bf16[1,1024,128]{2,1,0:T(8,128)(2,1)S(1)} %bitcast.60), channel_id=1, source_target_pairs={{0,16},{16,32},{32,48},{48,64},{64,80},{80,96},{96,112},{112,128},... | collective-permute-start | bytes 786440 | tf_op jit(solution)/shard_map/while/body/eval_jaxpr/ppermute | solution.py:17
  82.8 7.5 %collective-permute-start = (bf16[1,1024,128]{2,1,0:T(8,128)(2,1)S(1)}, bf16[1,1024,128]{2,1,0:T(8,128)(2,1)S(1)}, u32[]{:S(2)}, u32[]{:S(2)}) collective-permute-start(bf16[1,1024,128]{2,1,0:T(8,128)(2,1)S(1)} %get-tuple-element.627), channel_id=1, source_target_pairs={{1,0},{2,1},{3,2},{4,3},{5,4},{6,5},{7,6},{8,7},{9,8},{10,9},{11,1... | collective-permute-start | bytes 786440 | tf_op jit(solution)/shard_map/while/body/eval_jaxpr/ppermute | solution.py:20
  89.1 3.3 collective-permute-start.1
  92.5 7.9 %collective-permute-start.3 = (bf16[1,1024,128]{2,1,0:T(8,128)(2,1)S(1)}, bf16[1,1024,128]{2,1,0:T(8,128)(2,1)S(1)}, u32[]{:S(2)}, u32[]{:S(2)}) collective-permute-start(bf16[1,1024,128]{2,1,0:T(8,128)(2,1)S(1)} %bitcast.59), channel_id=1, source_target_pairs={{16,0},{32,16},{48,32},{64,48},{80,64},{96,80},{112,96},{128,112},... | collective-permute-start | bytes 786440 | tf_op jit(solution)/shard_map/while/body/eval_jaxpr/ppermute | solution.py:20
  93.8 8.0 %collective-permute-start.2 = (bf16[1,1024,128]{2,1,0:T(8,128)(2,1)S(1)}, bf16[1,1024,128]{2,1,0:T(8,128)(2,1)S(1)}, u32[]{:S(2)}, u32[]{:S(2)}) collective-permute-start(bf16[1,1024,128]{2,1,0:T(8,128)(2,1)S(1)} %bitcast.60), channel_id=1, source_target_pairs={{0,16},{16,32},{32,48},{48,64},{64,80},{80,96},{96,112},{112,128},... | collective-permute-start | bytes 786440 | tf_op jit(solution)/shard_map/while/body/eval_jaxpr/ppermute | solution.py:17
  106.4 7.4 %collective-permute-start = (bf16[1,1024,128]{2,1,0:T(8,128)(2,1)S(1)}, bf16[1,1024,128]{2,1,0:T(8,128)(2,1)S(1)}, u32[]{:S(2)}, u32[]{:S(2)}) collective-permute-start(bf16[1,1024,128]{2,1,0:T(8,128)(2,1)S(1)} %get-tuple-element.627), channel_id=1, source_target_pairs={{1,0},{2,1},{3,2},{4,3},{5,4},{6,5},{7,6},{8,7},{9,8},{10,9},{11,1... | collective-permute-start | bytes 786440 | tf_op jit(solution)/shard_map/while/body/eval_jaxpr/ppermute | solution.py:20
  112.3 3.3 collective-permute-start.1
  115.7 9.1 %collective-permute-start.3 = (bf16[1,1024,128]{2,1,0:T(8,128)(2,1)S(1)}, bf16[1,1024,128]{2,1,0:T(8,128)(2,1)S(1)}, u32[]{:S(2)}, u32[]{:S(2)}) collective-permute-start(bf16[1,1024,128]{2,1,0:T(8,128)(2,1)S(1)} %bitcast.59), channel_id=1, source_target_pairs={{16,0},{32,16},{48,32},{64,48},{80,64},{96,80},{112,96},{128,112},... | collective-permute-start | bytes 786440 | tf_op jit(solution)/shard_map/while/body/eval_jaxpr/ppermute | solution.py:20
  117.0 9.3 %collective-permute-start.2 = (bf16[1,1024,128]{2,1,0:T(8,128)(2,1)S(1)}, bf16[1,1024,128]{2,1,0:T(8,128)(2,1)S(1)}, u32[]{:S(2)}, u32[]{:S(2)}) collective-permute-start(bf16[1,1024,128]{2,1,0:T(8,128)(2,1)S(1)} %bitcast.60), channel_id=1, source_target_pairs={{0,16},{16,32},{32,48},{48,64},{64,80},{80,96},{96,112},{112,128},... | collective-permute-start | bytes 786440 | tf_op jit(solution)/shard_map/while/body/eval_jaxpr/ppermute | solution.py:17
  130.9 7.4 %collective-permute-start = (bf16[1,1024,128]{2,1,0:T(8,128)(2,1)S(1)}, bf16[1,1024,128]{2,1,0:T(8,128)(2,1)S(1)}, u32[]{:S(2)}, u32[]{:S(2)}) collective-permute-start(bf16[1,1024,128]{2,1,0:T(8,128)(2,1)S(1)} %get-tuple-element.627), channel_id=1, source_target_pairs={{1,0},{2,1},{3,2},{4,3},{5,4},{6,5},{7,6},{8,7},{9,8},{10,9},{11,1... | collective-permute-start | bytes 786440 | tf_op jit(solution)/shard_map/while/body/eval_jaxpr/ppermute | solution.py:20
  136.5 3.3 collective-permute-start.1
  140.0 10.2 %collective-permute-start.3 = (bf16[1,1024,128]{2,1,0:T(8,128)(2,1)S(1)}, bf16[1,1024,128]{2,1,0:T(8,128)(2,1)S(1)}, u32[]{:S(2)}, u32[]{:S(2)}) collective-permute-start(bf16[1,1024,128]{2,1,0:T(8,128)(2,1)S(1)} %bitcast.59), channel_id=1, source_target_pairs={{16,0},{32,16},{48,32},{64,48},{80,64},{96,80},{112,96},{128,112},... | collective-permute-start | bytes 786440 | tf_op jit(solution)/shard_map/while/body/eval_jaxpr/ppermute | solution.py:20
  141.3 10.4 %collective-permute-start.2 = (bf16[1,1024,128]{2,1,0:T(8,128)(2,1)S(1)}, bf16[1,1024,128]{2,1,0:T(8,128)(2,1)S(1)}, u32[]{:S(2)}, u32[]{:S(2)}) collective-permute-start(bf16[1,1024,128]{2,1,0:T(8,128)(2,1)S(1)} %bitcast.60), channel_id=1, source_target_pairs={{0,16},{16,32},{32,48},{48,64},{64,80},{80,96},{96,112},{112,128},... | collective-permute-start | bytes 786440 | tf_op jit(solution)/shard_map/while/body/eval_jaxpr/ppermute | solution.py:17
  156.2 7.4 %collective-permute-start = (bf16[1,1024,128]{2,1,0:T(8,128)(2,1)S(1)}, bf16[1,1024,128]{2,1,0:T(8,128)(2,1)S(1)}, u32[]{:S(2)}, u32[]{:S(2)}) collective-permute-start(bf16[1,1024,128]{2,1,0:T(8,128)(2,1)S(1)} %get-tuple-element.627), channel_id=1, source_target_pairs={{1,0},{2,1},{3,2},{4,3},{5,4},{6,5},{7,6},{8,7},{9,8},{10,9},{11,1... | collective-permute-start | bytes 786440 | tf_op jit(solution)/shard_map/while/body/eval_jaxpr/ppermute | solution.py:20
  161.7 3.3 collective-permute-start.1
  165.1 10.3 %collective-permute-start.3 = (bf16[1,1024,128]{2,1,0:T(8,128)(2,1)S(1)}, bf16[1,1024,128]{2,1,0:T(8,128)(2,1)S(1)}, u32[]{:S(2)}, u32[]{:S(2)}) collective-permute-start(bf16[1,1024,128]{2,1,0:T(8,128)(2,1)S(1)} %bitcast.59), channel_id=1, source_target_pairs={{16,0},{32,16},{48,32},{64,48},{80,64},{96,80},{112,96},{128,112},... | collective-permute-start | bytes 786440 | tf_op jit(solution)/shard_map/while/body/eval_jaxpr/ppermute | solution.py:20
  166.4 10.4 %collective-permute-start.2 = (bf16[1,1024,128]{2,1,0:T(8,128)(2,1)S(1)}, bf16[1,1024,128]{2,1,0:T(8,128)(2,1)S(1)}, u32[]{:S(2)}, u32[]{:S(2)}) collective-permute-start(bf16[1,1024,128]{2,1,0:T(8,128)(2,1)S(1)} %bitcast.60), channel_id=1, source_target_pairs={{0,16},{16,32},{32,48},{48,64},{64,80},{80,96},{96,112},{112,128},... | collective-permute-start | bytes 786440 | tf_op jit(solution)/shard_map/while/body/eval_jaxpr/ppermute | solution.py:17
  181.4 7.4 %collective-permute-start = (bf16[1,1024,128]{2,1,0:T(8,128)(2,1)S(1)}, bf16[1,1024,128]{2,1,0:T(8,128)(2,1)S(1)}, u32[]{:S(2)}, u32[]{:S(2)}) collective-permute-start(bf16[1,1024,128]{2,1,0:T(8,128)(2,1)S(1)} %get-tuple-element.627), channel_id=1, source_target_pairs={{1,0},{2,1},{3,2},{4,3},{5,4},{6,5},{7,6},{8,7},{9,8},{10,9},{11,1... | collective-permute-start | bytes 786440 | tf_op jit(solution)/shard_map/while/body/eval_jaxpr/ppermute | solution.py:20
  186.9 3.3 collective-permute-start.1
  190.3 10.2 %collective-permute-start.3 = (bf16[1,1024,128]{2,1,0:T(8,128)(2,1)S(1)}, bf16[1,1024,128]{2,1,0:T(8,128)(2,1)S(1)}, u32[]{:S(2)}, u32[]{:S(2)}) collective-permute-start(bf16[1,1024,128]{2,1,0:T(8,128)(2,1)S(1)} %bitcast.59), channel_id=1, source_target_pairs={{16,0},{32,16},{48,32},{64,48},{80,64},{96,80},{112,96},{128,112},... | collective-permute-start | bytes 786440 | tf_op jit(solution)/shard_map/while/body/eval_jaxpr/ppermute | solution.py:20
  191.6 10.4 %collective-permute-start.2 = (bf16[1,1024,128]{2,1,0:T(8,128)(2,1)S(1)}, bf16[1,1024,128]{2,1,0:T(8,128)(2,1)S(1)}, u32[]{:S(2)}, u32[]{:S(2)}) collective-permute-start(bf16[1,1024,128]{2,1,0:T(8,128)(2,1)S(1)} %bitcast.60), channel_id=1, source_target_pairs={{0,16},{16,32},{32,48},{48,64},{64,80},{80,96},{96,112},{112,128},... | collective-permute-start | bytes 786440 | tf_op jit(solution)/shard_map/while/body/eval_jaxpr/ppermute | solution.py:17
  206.6 7.4 %collective-permute-start = (bf16[1,1024,128]{2,1,0:T(8,128)(2,1)S(1)}, bf16[1,1024,128]{2,1,0:T(8,128)(2,1)S(1)}, u32[]{:S(2)}, u32[]{:S(2)}) collective-permute-start(bf16[1,1024,128]{2,1,0:T(8,128)(2,1)S(1)} %get-tuple-element.627), channel_id=1, source_target_pairs={{1,0},{2,1},{3,2},{4,3},{5,4},{6,5},{7,6},{8,7},{9,8},{10,9},{11,1... | collective-permute-start | bytes 786440 | tf_op jit(solution)/shard_map/while/body/eval_jaxpr/ppermute | solution.py:20
  212.0 3.3 collective-permute-start.1
  215.4 10.3 %collective-permute-start.3 = (bf16[1,1024,128]{2,1,0:T(8,128)(2,1)S(1)}, bf16[1,1024,128]{2,1,0:T(8,128)(2,1)S(1)}, u32[]{:S(2)}, u32[]{:S(2)}) collective-permute-start(bf16[1,1024,128]{2,1,0:T(8,128)(2,1)S(1)} %bitcast.59), channel_id=1, source_target_pairs={{16,0},{32,16},{48,32},{64,48},{80,64},{96,80},{112,96},{128,112},... | collective-permute-start | bytes 786440 | tf_op jit(solution)/shard_map/while/body/eval_jaxpr/ppermute | solution.py:20
  216.7 10.5 %collective-permute-start.2 = (bf16[1,1024,128]{2,1,0:T(8,128)(2,1)S(1)}, bf16[1,1024,128]{2,1,0:T(8,128)(2,1)S(1)}, u32[]{:S(2)}, u32[]{:S(2)}) collective-permute-start(bf16[1,1024,128]{2,1,0:T(8,128)(2,1)S(1)} %bitcast.60), channel_id=1, source_target_pairs={{0,16},{16,32},{32,48},{48,64},{64,80},{80,96},{96,112},{112,128},... | collective-permute-start | bytes 786440 | tf_op jit(solution)/shard_map/while/body/eval_jaxpr/ppermute | solution.py:17
  231.7 7.4 %collective-permute-start = (bf16[1,1024,128]{2,1,0:T(8,128)(2,1)S(1)}, bf16[1,1024,128]{2,1,0:T(8,128)(2,1)S(1)}, u32[]{:S(2)}, u32[]{:S(2)}) collective-permute-start(bf16[1,1024,128]{2,1,0:T(8,128)(2,1)S(1)} %get-tuple-element.627), channel_id=1, source_target_pairs={{1,0},{2,1},{3,2},{4,3},{5,4},{6,5},{7,6},{8,7},{9,8},{10,9},{11,1... | collective-permute-start | bytes 786440 | tf_op jit(solution)/shard_map/while/body/eval_jaxpr/ppermute | solution.py:20
  237.1 3.3 collective-permute-start.1
  240.5 10.2 %collective-permute-start.3 = (bf16[1,1024,128]{2,1,0:T(8,128)(2,1)S(1)}, bf16[1,1024,128]{2,1,0:T(8,128)(2,1)S(1)}, u32[]{:S(2)}, u32[]{:S(2)}) collective-permute-start(bf16[1,1024,128]{2,1,0:T(8,128)(2,1)S(1)} %bitcast.59), channel_id=1, source_target_pairs={{16,0},{32,16},{48,32},{64,48},{80,64},{96,80},{112,96},{128,112},... | collective-permute-start | bytes 786440 | tf_op jit(solution)/shard_map/while/body/eval_jaxpr/ppermute | solution.py:20
  241.8 10.4 %collective-permute-start.2 = (bf16[1,1024,128]{2,1,0:T(8,128)(2,1)S(1)}, bf16[1,1024,128]{2,1,0:T(8,128)(2,1)S(1)}, u32[]{:S(2)}, u32[]{:S(2)}) collective-permute-start(bf16[1,1024,128]{2,1,0:T(8,128)(2,1)S(1)} %bitcast.60), channel_id=1, source_target_pairs={{0,16},{16,32},{32,48},{48,64},{64,80},{80,96},{96,112},{112,128},... | collective-permute-start | bytes 786440 | tf_op jit(solution)/shard_map/while/body/eval_jaxpr/ppermute | solution.py:17
  256.8 7.4 %collective-permute-start = (bf16[1,1024,128]{2,1,0:T(8,128)(2,1)S(1)}, bf16[1,1024,128]{2,1,0:T(8,128)(2,1)S(1)}, u32[]{:S(2)}, u32[]{:S(2)}) collective-permute-start(bf16[1,1024,128]{2,1,0:T(8,128)(2,1)S(1)} %get-tuple-element.627), channel_id=1, source_target_pairs={{1,0},{2,1},{3,2},{4,3},{5,4},{6,5},{7,6},{8,7},{9,8},{10,9},{11,1... | collective-permute-start | bytes 786440 | tf_op jit(solution)/shard_map/while/body/eval_jaxpr/ppermute | solution.py:20
  262.1 3.3 collective-permute-start.1
  265.6 10.3 %collective-permute-start.3 = (bf16[1,1024,128]{2,1,0:T(8,128)(2,1)S(1)}, bf16[1,1024,128]{2,1,0:T(8,128)(2,1)S(1)}, u32[]{:S(2)}, u32[]{:S(2)}) collective-permute-start(bf16[1,1024,128]{2,1,0:T(8,128)(2,1)S(1)} %bitcast.59), channel_id=1, source_target_pairs={{16,0},{32,16},{48,32},{64,48},{80,64},{96,80},{112,96},{128,112},... | collective-permute-start | bytes 786440 | tf_op jit(solution)/shard_map/while/body/eval_jaxpr/ppermute | solution.py:20
  266.9 10.5 %collective-permute-start.2 = (bf16[1,1024,128]{2,1,0:T(8,128)(2,1)S(1)}, bf16[1,1024,128]{2,1,0:T(8,128)(2,1)S(1)}, u32[]{:S(2)}, u32[]{:S(2)}) collective-permute-start(bf16[1,1024,128]{2,1,0:T(8,128)(2,1)S(1)} %bitcast.60), channel_id=1, source_target_pairs={{0,16},{16,32},{32,48},{48,64},{64,80},{80,96},{96,112},{112,128},... | collective-permute-start | bytes 786440 | tf_op jit(solution)/shard_map/while/body/eval_jaxpr/ppermute | solution.py:17
  281.9 7.4 %collective-permute-start = (bf16[1,1024,128]{2,1,0:T(8,128)(2,1)S(1)}, bf16[1,1024,128]{2,1,0:T(8,128)(2,1)S(1)}, u32[]{:S(2)}, u32[]{:S(2)}) collective-permute-start(bf16[1,1024,128]{2,1,0:T(8,128)(2,1)S(1)} %get-tuple-element.627), channel_id=1, source_target_pairs={{1,0},{2,1},{3,2},{4,3},{5,4},{6,5},{7,6},{8,7},{9,8},{10,9},{11,1... | collective-permute-start | bytes 786440 | tf_op jit(solution)/shard_map/while/body/eval_jaxpr/ppermute | solution.py:20
  287.1 3.3 collective-permute-start.1
  290.6 10.3 %collective-permute-start.3 = (bf16[1,1024,128]{2,1,0:T(8,128)(2,1)S(1)}, bf16[1,1024,128]{2,1,0:T(8,128)(2,1)S(1)}, u32[]{:S(2)}, u32[]{:S(2)}) collective-permute-start(bf16[1,1024,128]{2,1,0:T(8,128)(2,1)S(1)} %bitcast.59), channel_id=1, source_target_pairs={{16,0},{32,16},{48,32},{64,48},{80,64},{96,80},{112,96},{128,112},... | collective-permute-start | bytes 786440 | tf_op jit(solution)/shard_map/while/body/eval_jaxpr/ppermute | solution.py:20
  291.9 10.5 %collective-permute-start.2 = (bf16[1,1024,128]{2,1,0:T(8,128)(2,1)S(1)}, bf16[1,1024,128]{2,1,0:T(8,128)(2,1)S(1)}, u32[]{:S(2)}, u32[]{:S(2)}) collective-permute-start(bf16[1,1024,128]{2,1,0:T(8,128)(2,1)S(1)} %bitcast.60), channel_id=1, source_target_pairs={{0,16},{16,32},{32,48},{48,64},{64,80},{80,96},{96,112},{112,128},... | collective-permute-start | bytes 786440 | tf_op jit(solution)/shard_map/while/body/eval_jaxpr/ppermute | solution.py:17
  306.9 7.4 %collective-permute-start = (bf16[1,1024,128]{2,1,0:T(8,128)(2,1)S(1)}, bf16[1,1024,128]{2,1,0:T(8,128)(2,1)S(1)}, u32[]{:S(2)}, u32[]{:S(2)}) collective-permute-start(bf16[1,1024,128]{2,1,0:T(8,128)(2,1)S(1)} %get-tuple-element.627), channel_id=1, source_target_pairs={{1,0},{2,1},{3,2},{4,3},{5,4},{6,5},{7,6},{8,7},{9,8},{10,9},{11,1... | collective-permute-start | bytes 786440 | tf_op jit(solution)/shard_map/while/body/eval_jaxpr/ppermute | solution.py:20
  312.2 3.3 collective-permute-start.1
  315.6 10.3 %collective-permute-start.3 = (bf16[1,1024,128]{2,1,0:T(8,128)(2,1)S(1)}, bf16[1,1024,128]{2,1,0:T(8,128)(2,1)S(1)}, u32[]{:S(2)}, u32[]{:S(2)}) collective-permute-start(bf16[1,1024,128]{2,1,0:T(8,128)(2,1)S(1)} %bitcast.59), channel_id=1, source_target_pairs={{16,0},{32,16},{48,32},{64,48},{80,64},{96,80},{112,96},{128,112},... | collective-permute-start | bytes 786440 | tf_op jit(solution)/shard_map/while/body/eval_jaxpr/ppermute | solution.py:20
  316.9 10.5 %collective-permute-start.2 = (bf16[1,1024,128]{2,1,0:T(8,128)(2,1)S(1)}, bf16[1,1024,128]{2,1,0:T(8,128)(2,1)S(1)}, u32[]{:S(2)}, u32[]{:S(2)}) collective-permute-start(bf16[1,1024,128]{2,1,0:T(8,128)(2,1)S(1)} %bitcast.60), channel_id=1, source_target_pairs={{0,16},{16,32},{32,48},{48,64},{64,80},{80,96},{96,112},{112,128},... | collective-permute-start | bytes 786440 | tf_op jit(solution)/shard_map/while/body/eval_jaxpr/ppermute | solution.py:17
  331.9 7.4 %collective-permute-start = (bf16[1,1024,128]{2,1,0:T(8,128)(2,1)S(1)}, bf16[1,1024,128]{2,1,0:T(8,128)(2,1)S(1)}, u32[]{:S(2)}, u32[]{:S(2)}) collective-permute-start(bf16[1,1024,128]{2,1,0:T(8,128)(2,1)S(1)} %get-tuple-element.627), channel_id=1, source_target_pairs={{1,0},{2,1},{3,2},{4,3},{5,4},{6,5},{7,6},{8,7},{9,8},{10,9},{11,1... | collective-permute-start | bytes 786440 | tf_op jit(solution)/shard_map/while/body/eval_jaxpr/ppermute | solution.py:20
  337.1 3.3 collective-permute-start.1
  340.5 10.3 %collective-permute-start.3 = (bf16[1,1024,128]{2,1,0:T(8,128)(2,1)S(1)}, bf16[1,1024,128]{2,1,0:T(8,128)(2,1)S(1)}, u32[]{:S(2)}, u32[]{:S(2)}) collective-permute-start(bf16[1,1024,128]{2,1,0:T(8,128)(2,1)S(1)} %bitcast.59), channel_id=1, source_target_pairs={{16,0},{32,16},{48,32},{64,48},{80,64},{96,80},{112,96},{128,112},... | collective-permute-start | bytes 786440 | tf_op jit(solution)/shard_map/while/body/eval_jaxpr/ppermute | solution.py:20
  341.8 10.4 %collective-permute-start.2 = (bf16[1,1024,128]{2,1,0:T(8,128)(2,1)S(1)}, bf16[1,1024,128]{2,1,0:T(8,128)(2,1)S(1)}, u32[]{:S(2)}, u32[]{:S(2)}) collective-permute-start(bf16[1,1024,128]{2,1,0:T(8,128)(2,1)S(1)} %bitcast.60), channel_id=1, source_target_pairs={{0,16},{16,32},{32,48},{48,64},{64,80},{80,96},{96,112},{112,128},... | collective-permute-start | bytes 786440 | tf_op jit(solution)/shard_map/while/body/eval_jaxpr/ppermute | solution.py:17
  356.8 7.4 %collective-permute-start = (bf16[1,1024,128]{2,1,0:T(8,128)(2,1)S(1)}, bf16[1,1024,128]{2,1,0:T(8,128)(2,1)S(1)}, u32[]{:S(2)}, u32[]{:S(2)}) collective-permute-start(bf16[1,1024,128]{2,1,0:T(8,128)(2,1)S(1)} %get-tuple-element.627), channel_id=1, source_target_pairs={{1,0},{2,1},{3,2},{4,3},{5,4},{6,5},{7,6},{8,7},{9,8},{10,9},{11,1... | collective-permute-start | bytes 786440 | tf_op jit(solution)/shard_map/while/body/eval_jaxpr/ppermute | solution.py:20
  362.0 3.3 collective-permute-start.1
  365.4 10.3 %collective-permute-start.3 = (bf16[1,1024,128]{2,1,0:T(8,128)(2,1)S(1)}, bf16[1,1024,128]{2,1,0:T(8,128)(2,1)S(1)}, u32[]{:S(2)}, u32[]{:S(2)}) collective-permute-start(bf16[1,1024,128]{2,1,0:T(8,128)(2,1)S(1)} %bitcast.59), channel_id=1, source_target_pairs={{16,0},{32,16},{48,32},{64,48},{80,64},{96,80},{112,96},{128,112},... | collective-permute-start | bytes 786440 | tf_op jit(solution)/shard_map/while/body/eval_jaxpr/ppermute | solution.py:20
  366.7 10.5 %collective-permute-start.2 = (bf16[1,1024,128]{2,1,0:T(8,128)(2,1)S(1)}, bf16[1,1024,128]{2,1,0:T(8,128)(2,1)S(1)}, u32[]{:S(2)}, u32[]{:S(2)}) collective-permute-start(bf16[1,1024,128]{2,1,0:T(8,128)(2,1)S(1)} %bitcast.60), channel_id=1, source_target_pairs={{0,16},{16,32},{32,48},{48,64},{64,80},{80,96},{96,112},{112,128},... | collective-permute-start | bytes 786440 | tf_op jit(solution)/shard_map/while/body/eval_jaxpr/ppermute | solution.py:17
  381.7 7.4 %collective-permute-start = (bf16[1,1024,128]{2,1,0:T(8,128)(2,1)S(1)}, bf16[1,1024,128]{2,1,0:T(8,128)(2,1)S(1)}, u32[]{:S(2)}, u32[]{:S(2)}) collective-permute-start(bf16[1,1024,128]{2,1,0:T(8,128)(2,1)S(1)} %get-tuple-element.627), channel_id=1, source_target_pairs={{1,0},{2,1},{3,2},{4,3},{5,4},{6,5},{7,6},{8,7},{9,8},{10,9},{11,1... | collective-permute-start | bytes 786440 | tf_op jit(solution)/shard_map/while/body/eval_jaxpr/ppermute | solution.py:20
  390.3 10.3 %collective-permute-start.3 = (bf16[1,1024,128]{2,1,0:T(8,128)(2,1)S(1)}, bf16[1,1024,128]{2,1,0:T(8,128)(2,1)S(1)}, u32[]{:S(2)}, u32[]{:S(2)}) collective-permute-start(bf16[1,1024,128]{2,1,0:T(8,128)(2,1)S(1)} %bitcast.59), channel_id=1, source_target_pairs={{16,0},{32,16},{48,32},{64,48},{80,64},{96,80},{112,96},{128,112},... | collective-permute-start | bytes 786440 | tf_op jit(solution)/shard_map/while/body/eval_jaxpr/ppermute | solution.py:20
  391.6 10.4 %collective-permute-start.2 = (bf16[1,1024,128]{2,1,0:T(8,128)(2,1)S(1)}, bf16[1,1024,128]{2,1,0:T(8,128)(2,1)S(1)}, u32[]{:S(2)}, u32[]{:S(2)}) collective-permute-start(bf16[1,1024,128]{2,1,0:T(8,128)(2,1)S(1)} %bitcast.60), channel_id=1, source_target_pairs={{0,16},{16,32},{32,48},{48,64},{64,80},{80,96},{96,112},{112,128},... | collective-permute-start | bytes 786440 | tf_op jit(solution)/shard_map/while/body/eval_jaxpr/ppermute | solution.py:17
  (2 other events, 3.9 us)
Sparse Core Ops, SparseCore 0:
  403.2 145.4 all-gather.2
